TPU v7x, 32 devices: a whole 2x2x4 slice. The times are simulated.
32 devices in a mesh: req: 16 (over z, x, core), ep: 2 (over y).
Axes of the slice: x: 2, y: 2, z: 4, core: 2. Of those that a mesh axis runs over, the one named last changes fastest.
Arguments:
- hidden: bfloat16 [16, 512, 1536], P('req', None, 'ep'), may hold values from -6 to 6
- key_cache: bfloat16 [16, 8, 2560, 64], P('req', 'ep'), may hold values from -160 to 160
- value_cache: bfloat16 [16, 8, 2560, 64], P('req', 'ep'), may hold values from -6 to 6
- request_order: int32 [16], replicated, may hold values from 0 to 15, each once
- cached_lengths: int32 [16], replicated, may hold values from 1 to 2048, 16384 in all
- expert_ids: int32 [16, 512, 8], P('req'), may hold values from 0 to 39, all different within a row; in each aligned block of 512 rows (0 to 511, 512 to 1023, ..., all dimensions but the last counted through in order) at most 192 rows name the same one
- gate_values: float32 [16, 512, 8], P('req'), may hold values from 0.1 to 1
- attn_gain: float32 [1536], replicated, may hold values from 0.25 to 1.75
- ffn_gain: float32 [1536], replicated, may hold values from 0.25 to 1.75
- w_query: bfloat16 [1536, 1536], P(None, 'ep'), may hold values from -0.15625 to 0.15625
- w_key: bfloat16 [1536, 512], P(None, 'ep'), may hold values from -0.15625 to 0.15625
- w_value: bfloat16 [1536, 512], P(None, 'ep'), may hold values from -0.15625 to 0.15625
- w_out: bfloat16 [1536, 1536], P('ep'), may hold values from -0.15625 to 0.15625
- expert_gate: bfloat16 [4, 1536, 512], P('ep', 'req'), may hold values from -0.15625 to 0.15625
- expert_up: bfloat16 [4, 1536, 512], P('ep', 'req'), may hold values from -0.15625 to 0.15625
- expert_down: bfloat16 [4, 512, 1536], P('ep', 'req'), may hold values from -0.25 to 0.25
Outputs:
- hidden_out: bfloat16 [16, 512, 1536], P('req', None, 'ep')
- key_cache_out: bfloat16 [16, 8, 2560, 64], P('req', 'ep')
- value_cache_out: bfloat16 [16, 8, 2560, 64], P('req', 'ep')
Inputs may be any that keep to these rules, and one draw needn't show every extreme that they name: Slot s holds request request_order[s]; every request is held by one slot. `cached_lengths`: the longest cached length is exactly 2048. `expert_ids`: each token names 8 different experts; among the 512 tokens of one slot no expert is named by more than 192 tokens, a bound that some block reaches.
All inputs are finite; a program needn't handle non-finite values.
Results may differ from a plain program's by a relative error of at most 0.012.
The roundings to bfloat16 on the way count: a program that leaves them out, or rounds other values in their place, can miss the bound.
Values may be sent and summed in bfloat16 or wider, within the bound.
No kernel may reach another device: no remote copies, remote signals or barrier semaphores. Data moves between devices by JAX's collectives and lax.ppermute only.
A program may use at most 128 MiB of HBM per device.

v0:
```python
import jax
import jax.numpy as jnp
from jax import lax
from jax.experimental import pallas as pl
from jax.experimental.pallas import tpu as pltpu
from jax.sharding import PartitionSpec as P

epsilon = 1e-06


def normalize(values, gain):
    return values * lax.rsqrt(jnp.mean(values * values, -1, keepdims=True) + epsilon) * gain


def rotate(values, positions):
    half = values.shape[-1] // 2
    freq = 10000.0 ** (-jnp.arange(half, dtype=jnp.float32) * (2.0 / values.shape[-1]))
    angle = positions.astype(jnp.float32)[:, None] * freq[None, :]
    cosine = jnp.cos(angle)
    sine = jnp.sin(angle)
    first = values[..., :half]
    second = values[..., half:]
    return jnp.concatenate([first * cosine - second * sine, second * cosine + first * sine], -1)


def rounded(values):
    return lax.optimization_barrier(values.astype(jnp.bfloat16)).astype(jnp.float32)


def route_tables(chosen, gate_rows, wanted, capacity):
    hits = chosen[:, :, None] == wanted[None, None, :]
    member = jnp.sum(hits.astype(jnp.int32), 1, dtype=jnp.int32)
    weight = jnp.sum(jnp.where(hits, gate_rows[:, :, None], 0.0), 1)
    place = jnp.cumsum(member, 0, dtype=jnp.int32) - 1
    slots = jnp.arange(capacity, dtype=jnp.int32)
    table = (member.T[:, None, :] == 1) & (place.T[:, None, :] == slots[None, :, None])
    gate_slot = jnp.sum(jnp.where(table, weight.T[:, None, :], 0.0), 2)
    return (table.astype(jnp.bfloat16), gate_slot)


def flash_attend(query, keys, values, key_new, value_new, length, first_token, tokens):
    kv_heads, rows, head_dim = query.shape
    block = key_new.shape[2]
    cached = keys.shape[2] - block
    wide = cached if cached % block == 0 else block
    blocks = 1 + cached // wide

    def cached_blocks(length_ref):
        return (length_ref[0] + wide - 1) // wide

    def kernel(length_ref, q_ref, kc_ref, vc_ref, kn_ref, vn_ref, o_ref, m_sc, l_sc, acc_sc):
        step = pl.program_id(1)
        length = length_ref[0]

        def visit(key_block, value_block, visible, first):
            scores = jnp.dot(q_ref[0], key_block, preferred_element_type=jnp.float32)
            if visible is not None:
                scores = jnp.where(visible, scores, -1e30)
            if first:
                highest = jnp.max(scores, -1, keepdims=True)
            else:
                previous = m_sc[...]
                highest = jnp.maximum(previous, jnp.max(scores, -1, keepdims=True))
            probs = jnp.exp(scores - highest)
            if visible is not None:
                probs = jnp.where(visible, probs, 0.0)
            summed = lax.dot_general(
                probs.astype(jnp.bfloat16),
                value_block,
                (((1,), (1,)), ((), ())),
                preferred_element_type=jnp.float32,
            )
            if first:
                l_sc[...] = jnp.sum(probs, -1, keepdims=True)
                acc_sc[...] = summed
            else:
                correction = jnp.exp(previous - highest)
                l_sc[...] = l_sc[...] * correction + jnp.sum(probs, -1, keepdims=True)
                acc_sc[...] = acc_sc[...] * correction + summed
            m_sc[...] = highest

        @pl.when(step == 0)
        def _():
            shape = (rows, block)
            column = lax.broadcasted_iota(jnp.int32, shape, 1)
            token = first_token + lax.rem(lax.broadcasted_iota(jnp.int32, shape, 0), tokens)
            visit(kn_ref[0], vn_ref[0], column <= token, True)

        column = lax.broadcasted_iota(jnp.int32, (rows, wide), 1)
        start = (step - 1) * wide

        whole = (step > 0) & (start + wide <= length)

        @pl.when(whole)
        def _():
            visit(kc_ref[0], vc_ref[0], None, False)

        @pl.when((step > 0) & jnp.logical_not(whole) & (start < length))
        def _():
            visit(kc_ref[0], vc_ref[0], column + start < length, False)

        @pl.when(step == blocks - 1)
        def _():
            o_ref[0] = (acc_sc[...] / l_sc[...]).astype(o_ref.dtype)

    def cache_map(head, step, length_ref):
        return (head, 0, jnp.clip(step - 1, 0, cached_blocks(length_ref) - 1))

    def fixed_map(head, step, length_ref):
        return (head, 0, 0)

    grid_spec = pltpu.PrefetchScalarGridSpec(
        num_scalar_prefetch=1,
        grid=(kv_heads, blocks),
        in_specs=[
            pl.BlockSpec((1, rows, head_dim), fixed_map),
            pl.BlockSpec((1, head_dim, wide), cache_map),
            pl.BlockSpec((1, head_dim, wide), cache_map),
            pl.BlockSpec((1, head_dim, block), fixed_map),
            pl.BlockSpec((1, head_dim, block), fixed_map),
        ],
        out_specs=pl.BlockSpec((1, rows, head_dim), fixed_map),
        scratch_shapes=[
            pltpu.VMEM((rows, 1), jnp.float32),
            pltpu.VMEM((rows, 1), jnp.float32),
            pltpu.VMEM((rows, head_dim), jnp.float32),
        ],
    )
    flops = 4 * kv_heads * rows * keys.shape[2] * head_dim
    return pl.pallas_call(
        kernel,
        grid_spec=grid_spec,
        out_shape=jax.ShapeDtypeStruct(query.shape, jnp.bfloat16),
        compiler_params=pltpu.CompilerParams(dimension_semantics=("arbitrary", "arbitrary")),
        cost_estimate=pl.CostEstimate(
            flops=flops,
            transcendentals=kv_heads * rows * keys.shape[2],
            bytes_accessed=2 * (query.size + keys.size + values.size + query.size),
        ),
    )(length.reshape(1), query, keys, values, key_new, value_new)


def shifted(values, shift):
    devices = lax.axis_size("ep")
    return lax.ppermute(values, "ep", [(i, (i + shift) % devices) for i in range(devices)])


def gather_columns(values):
    devices = lax.axis_size("ep")
    me = lax.axis_index("ep")
    width = values.shape[-1]
    whole = jnp.zeros(values.shape[:-1] + (width * devices,), values.dtype)
    for shift in range(devices):
        piece = values if shift == 0 else shifted(values, shift)
        source = (me - shift) % devices
        whole = lax.dynamic_update_slice_in_dim(whole, piece, source * width, values.ndim - 1)
    return whole


def sum_over_ep(part):
    devices = lax.axis_size("ep")
    total = part.astype(jnp.float32)
    for shift in range(1, devices):
        total = total + shifted(part, shift).astype(jnp.float32)
    return total


def on_device(
    hidden,
    key_cache,
    value_cache,
    request_order,
    cached_lengths,
    expert_ids,
    gate_values,
    attn_gain,
    ffn_gain,
    w_query,
    w_key,
    w_value,
    w_out,
    expert_gate,
    expert_up,
    expert_down,
):
    own_rows = hidden[0]
    new_rows = own_rows.shape[0]
    own_width = own_rows.shape[1]
    head_dim = key_cache.shape[3]
    kv_local = key_cache.shape[1]
    heads_local = w_query.shape[1] // head_dim
    group = heads_local // kv_local
    per_device = expert_gate.shape[0]
    capacity = 3 * new_rows // 8
    me = lax.axis_index("ep")
    gate_up = lax.all_gather(jnp.stack([expert_gate, expert_up]), "req", axis=2, tiled=True)
    gate_whole = gate_up[0]
    up_whole = gate_up[1]
    down_whole = lax.all_gather(expert_down, "req", axis=1, tiled=True)
    everyone = jnp.arange(request_order.shape[0], dtype=jnp.int32)
    request = jnp.sum(jnp.where(everyone == lax.axis_index("req"), request_order, 0))
    length = jnp.sum(jnp.where(everyone == request, cached_lengths, 0))
    rows_whole = gather_columns(own_rows)
    rows_f = rows_whole.astype(jnp.float32)
    normed = normalize(rows_f, attn_gain).astype(jnp.bfloat16)
    query = jnp.dot(normed, w_query, preferred_element_type=jnp.float32)
    key_new = jnp.dot(normed, w_key, preferred_element_type=jnp.float32)
    value_new = jnp.dot(normed, w_value, preferred_element_type=jnp.float32)
    positions = length + jnp.arange(new_rows, dtype=jnp.int32)
    query = rotate(
        query.reshape(new_rows, heads_local, head_dim).transpose(1, 0, 2), positions
    ).astype(jnp.bfloat16) * jnp.asarray(head_dim ** (-0.5), jnp.bfloat16)
    key_new = rotate(
        key_new.reshape(new_rows, kv_local, head_dim).transpose(1, 0, 2), positions
    ).astype(jnp.bfloat16)
    value_new = (
        value_new.reshape(new_rows, kv_local, head_dim).transpose(1, 0, 2).astype(jnp.bfloat16)
    )
    zero = jnp.zeros((), jnp.int32)
    keys = lax.dynamic_update_slice(key_cache[0], key_new, (zero, length, zero))
    values = lax.dynamic_update_slice(value_cache[0], value_new, (zero, length, zero))
    half = new_rows // 2
    query = query.reshape(kv_local, group, new_rows, head_dim)
    key_cache_t = jnp.swapaxes(key_cache[0], 1, 2)
    value_cache_t = jnp.swapaxes(value_cache[0], 1, 2)
    key_new_t = jnp.swapaxes(key_new, 1, 2)
    value_new_t = jnp.swapaxes(value_new, 1, 2)
    head_sums = []
    for first in (0, half):
        part_query = query[:, :, first : first + half].reshape(kv_local, group * half, head_dim)
        attended = flash_attend(
            part_query,
            key_cache_t,
            value_cache_t,
            key_new_t,
            value_new_t,
            length,
            first,
            half,
        )
        attended = (
            attended.reshape(heads_local, half, head_dim)
            .transpose(1, 0, 2)
            .reshape(half, heads_local * head_dim)
        )
        head_part = jnp.dot(attended, w_out, preferred_element_type=jnp.float32).astype(
            jnp.bfloat16
        )
        head_sums.append(sum_over_ep(head_part))
    head_sum = jnp.concatenate(head_sums, 0)
    mixed_f = (rows_f + head_sum).astype(jnp.bfloat16).astype(jnp.float32)
    ffn_normed = normalize(mixed_f, ffn_gain).astype(jnp.bfloat16)
    table, gate_slot = route_tables(
        expert_ids[0],
        gate_values[0],
        me * per_device + jnp.arange(per_device, dtype=jnp.int32),
        capacity,
    )
    dispatched = jnp.einsum(
        "ect,td->ecd", table, ffn_normed, preferred_element_type=jnp.float32
    ).astype(jnp.bfloat16)
    gate_whole, up_whole, dispatched = lax.optimization_barrier((gate_whole, up_whole, dispatched))
    gate_act = jnp.einsum("ecd,edf->ecf", dispatched, gate_whole, preferred_element_type=jnp.float32)
    up_act = jnp.einsum("ecd,edf->ecf", dispatched, up_whole, preferred_element_type=jnp.float32)
    act = (jax.nn.silu(gate_act) * up_act).astype(jnp.bfloat16)
    down_whole, act = lax.optimization_barrier((down_whole, act))
    devices = lax.axis_size("ep")

    def expert_block(target):
        down_block = lax.dynamic_slice_in_dim(down_whole, target * own_width, own_width, 2)
        output = jnp.einsum("ecf,efd->ecd", act, down_block, preferred_element_type=jnp.float32)
        contrib = (output * gate_slot[..., None]).astype(jnp.bfloat16)
        return jnp.einsum(
            "ect,ecd->td", table, contrib, preferred_element_type=jnp.float32
        ).astype(jnp.bfloat16)

    received = [shifted(expert_block((me + shift) % devices), shift) for shift in range(1, devices)]
    expert_sum = expert_block(me).astype(jnp.float32)
    for piece in received:
        expert_sum = expert_sum + piece.astype(jnp.float32)
    mixed_own = lax.dynamic_slice_in_dim(mixed_f, me * own_width, own_width, 1)
    result = (mixed_own + expert_sum).astype(jnp.bfloat16)
    return (result[None], keys[None], values[None])


def solution(mesh):
    in_specs = (
        P("req", None, "ep"),
        P("req", "ep", None, None),
        P("req", "ep", None, None),
        P(),
        P(),
        P("req", None, None),
        P("req", None, None),
        P(),
        P(),
        P(None, "ep"),
        P(None, "ep"),
        P(None, "ep"),
        P("ep", None),
        P("ep", "req", None),
        P("ep", "req", None),
        P("ep", "req", None),
    )
    out_specs = (P("req", None, "ep"), P("req", "ep", None, None), P("req", "ep", None, None))
    return jax.shard_map(
        on_device, mesh=mesh, in_specs=in_specs, out_specs=out_specs, check_vma=False
    )
```

profile of v0, /device:TPU:16, one launch (start us, length us, event | category | flops | bytes accessed | tf_op | source)
XLA Modules:
  0.0 155.5 jit_solution(10795286882972518527)
XLA Ops:
  7.2 0.0 all-gather.5.cloned.1.call-start
  7.2 2.6 %copy.47 = bf16[1,4,2560,64]{2,3,1,0:T(8,128)(2,1)} copy(bf16[1,4,2560,64]{2,3,1,0:T(8,128)(2,1)} %param.17) | data formatting | bytes 2621440
  9.9 1.1 copy.48
  11.0 0.2 copy-done.13
  11.2 0.8 pad_maximum_fusion
  12.0 0.0 all-gather.3.cloned.1.call-start
  12.0 1.6 %collective-permute-start = (bf16[512,768]{1,0:T(8,128)(2,1)S(1)}, bf16[512,768]{1,0:T(8,128)(2,1)}, u32[]{:S(2)}, u32[]{:S(2)}) collective-permute-start(bf16[512,768]{1,0:T(8,128)(2,1)S(1)} %bitcast.92), channel_id=1, source_target_pairs={{0,1},{1,0},{2,3},{3,2},{4,5},{5,4},{6,7},{7,6},{8,9},{9,8},{10,11... | collective-permute-start | bytes 2359304 | tf_op jit(solution)/shard_map/ppermute | solution.py:145
  13.7 0.6 fusion.49
  14.4 1.3 fusion.50
  15.7 0.7 add_convert_fusion.3
  16.4 0.1 fusion.43
  16.5 0.6 copy-done.15
  17.1 0.6 reduce-window.6
  17.7 0.2 slice_reduce_fusion
  17.9 0.2 reduce-window.9
  18.1 0.7 add_bitcast_fusion
  18.8 0.3 multiply_cosine_fusion
  19.1 0.1 broadcast_in_dim.33
  19.2 0.1 constant_dynamic-update-slice_fusion.1
  19.3 12.2 %collective-permute-done = bf16[512,768]{1,0:T(8,128)(2,1)} collective-permute-done((bf16[512,768]{1,0:T(8,128)(2,1)S(1)}, bf16[512,768]{1,0:T(8,128)(2,1)}, u32[]{:S(2)}, u32[]{:S(2)}) %collective-permute-start) | collective-permute-done | bytes 786464 | tf_op jit(solution)/shard_map/ppermute | solution.py:145
  31.5 1.2 constant_dynamic-update-slice_fusion
  32.7 0.4 fusion
  33.1 0.8 fusion.52
  33.9 1.0 copy-done.25
  34.9 1.6 fusion.54
  36.5 0.1 subtract_convert_fusion.1
  36.6 0.3 subtract_convert_fusion
  36.9 1.5 copy.34
  38.4 1.5 copy.33
  39.9 0.7 maximum_bitcast_fusion.kn_ref
  40.6 2.8 %maximum_multiply_fusion = bf16[4,3,512,64]{3,2,1,0:T(8,128)(2,1)S(1)} fusion(bf16[4,3,512,32]{3,2,1,0:T(8,128)(2,1)} %copy.34, bf16[4,3,512,32]{3,2,1,0:T(8,128)(2,1)} %copy.33), kind=kLoop, calls=%fused_computation.16 | loop fusion | flops 2359296 | bytes 1572864 | tf_op jit(solution)/shard_map/mul | solution.py:210
  43.5 1.2 fusion.57
  44.7 0.7 copy-done.2
  45.5 0.2 copy-done.27
  45.7 1.5 convolution_convert_fusion.3
  47.1 17.8 %shard_map.175 = bf16[4,768,64]{2,1,0:T(8,128)(2,1)} custom-call(s32[1]{0:T(128)} %bitcast.1.length_ref, bf16[4,768,64]{2,1,0:T(8,128)(2,1)} %bitcast.96, bf16[4,64,2560]{2,1,0:T(8,128)(2,1)} %bitcast.86, bf16[4,64,2560]{2,1,0:T(8,128)(2,1)} %bitcast.88, bf16[4,64,512]{2,1,0:T(8,128)(2,1)} %maximum_bitcast_fusion.kn_ref, bf16[4,64,512]{2,1,0:T(8,128)(2,1)} %bitcast.98), custom_call_target="tpu_custom_call" | custom-call | flops 2013265920 | bytes 3407872 | tf_op jit(solution)/shard_map/pallas_call | solution.py:130
  65.0 1.4 copy.35
  66.4 0.8 convolution_convert_fusion.2
  67.2 1.6 %collective-permute-start.1 = (bf16[256,1536]{1,0:T(8,128)(2,1)S(1)}, bf16[256,1536]{1,0:T(8,128)(2,1)}, u32[]{:S(2)}, u32[]{:S(2)}) collective-permute-start(bf16[256,1536]{1,0:T(8,128)(2,1)S(1)} %convolution_convert_fusion.2), channel_id=1, source_target_pairs={{0,1},{1,0},{2,3},{3,2},{4,5},{5,4},{6,7},{7,6},{8,9},{9,8},{10,11... | collective-permute-start | bytes 2359304 | tf_op jit(solution)/shard_map/ppermute | solution.py:145
  68.8 0.6 broadcast_compare_fusion
  69.4 1.3 copy.40
  70.6 18.3 %shard_map.176 = bf16[4,768,64]{2,1,0:T(8,128)(2,1)} custom-call(s32[1]{0:T(128)} %bitcast.1.length_ref, bf16[4,768,64]{2,1,0:T(8,128)(2,1)} %bitcast.95, bf16[4,64,2560]{2,1,0:T(8,128)(2,1)} %bitcast.87, bf16[4,64,2560]{2,1,0:T(8,128)(2,1)} %bitcast.89, bf16[4,64,512]{2,1,0:T(8,128)(2,1)} %maximum_bitcast_fusion.kn_ref, bf16[4,64,512]{2,1,0:T(8,128)(2,1)} %bitcast.99), custom_call_target="tpu_custom_call" | custom-call | flops 2013265920 | bytes 3407872 | tf_op jit(solution)/shard_map/pallas_call | solution.py:130
  88.9 1.4 copy.36
  90.4 0.8 convolution_convert_fusion.1
  91.2 0.5 collective-permute-start.2
  91.7 0.1 fusion.44
  91.8 0.2 select_reduce_fusion
  92.1 1.3 convert_add_fusion.2
  93.4 16.2 %collective-permute-done.2 = bf16[256,1536]{1,0:T(8,128)(2,1)S(1)} collective-permute-done((bf16[256,1536]{1,0:T(8,128)(2,1)S(1)}, bf16[256,1536]{1,0:T(8,128)(2,1)S(1)}, u32[]{:S(2)}, u32[]{:S(2)}) %collective-permute-start.2) | collective-permute-done | bytes 786464 | tf_op jit(solution)/shard_map/ppermute | solution.py:145
  109.7 0.2 convert_add_fusion.1
  109.9 0.5 multiply_reduce_fusion
  110.4 1.6 %copy-done.4 = f32[512,1536]{1,0:T(8,128)} copy-done((f32[512,1536]{1,0:T(8,128)}, f32[512,1536]{1,0:T(8,128)S(1)}, u32[]{:S(2)}) %copy-start.4) | copy-done | bytes 3145752
  112.1 1.0 convolution_convert_fusion
  113.0 0.0 all-gather.5.cloned.1.call-done
  113.1 3.4 %slice_bitcast_fusion = (bf16[2,1536,512]{2,1,0:T(8,128)(2,1)S(1)}, bf16[2,1536,512]{2,1,0:T(8,128)(2,1)S(1)}) fusion(bf16[2,2,1536,512]{3,2,1,0:T(8,128)(2,1)} %all-gather.5.cloned.1.call-done), kind=kLoop, calls=%fused_computation.7 | loop fusion | bytes 12582912 | tf_op jit(solution)/shard_map/squeeze | solution.py:198
  116.4 0.8 fusion.58
  117.2 1.6 %fusion.28 = bf16[2,192,512]{2,1,0:T(8,128)(2,1)} fusion(bf16[2,192,1536]{2,1,0:T(8,128)(2,1)S(1)} %convolution_convert_fusion, bf16[2,1536,512]{2,1,0:T(8,128)(2,1)S(1)} %get-tuple-element.10, f32[2,192,512]{2,1,0:T(8,128)S(1)} %fusion.58), kind=kOutput, calls=%fused_computation.34 | convolution fusion | flops 605159424 | bytes 5505024 | tf_op jit(solution)/shard_map/ecd,edf->ecf/dot_general | solution.py:264
  118.8 2.5 %all-gather.3.cloned.1.call-done = bf16[2,512,1536]{2,1,0:T(8,128)(2,1)} async-done(((bf16[2,32,1536]{2,1,0:T(8,128)(2,1)}), bf16[2,512,1536]{2,1,0:T(8,128)(2,1)}) %all-gather.3.cloned.1.call-update) | async-done | bytes 3145744 | tf_op jit(solution)/shard_map/all_gather | solution.py:199
  121.3 3.4 %bitcast_convert_fusion = bf16[512,768]{1,0:T(8,128)(2,1)} fusion(bf16[2,192,512]{2,1,0:T(8,128)(2,1)} %fusion.28, bf16[2,512,1536]{2,1,0:T(8,128)(2,1)} %all-gather.3.cloned.1.call-done, s32[]{:T(128)S(6)} %select_n.57, f32[2,192]{1,0:T(2,128)S(1)} %select_reduce_fusion, s32[2,512]{1,0:T(2,128)S(1)} %bitcast.108, pred[2,512]{1,0:T(4,128)(4,1)S(1)} %copy-done.20), kind=kOutput, calls=%fused_computation.17 | convolution fusion | flops 605356032 | bytes 2759172 | tf_op jit(solution)/shard_map/ect,ecd->td/dot_general | solution.py:273
  124.7 1.5 collective-permute-start.3
  128.1 2.8 %dynamic_update_slice.17 = bf16[1,4,2560,64]{2,3,1,0:T(8,128)(2,1)} dynamic-update-slice(bf16[1,4,2560,64]{2,3,1,0:T(8,128)(2,1)} %copy.48, bf16[1,4,512,64]{2,3,1,0:T(8,128)(2,1)S(1)} %bitcast.100, s32[]{:T(128)} %constant.50.clone.1, s32[]{:T(128)} %constant.50.clone.1, s32[]{:T(128)S(6)} %select_n.58, s32[]{:T(128)} %constant.50.clone.1) | dynamic-update-slice | bytes 524292 | tf_op jit(solution)/shard_map/dynamic_update_slice | solution.py:221
  130.9 2.8 %dynamic_update_slice.16 = bf16[1,4,2560,64]{2,3,1,0:T(8,128)(2,1)} dynamic-update-slice(bf16[1,4,2560,64]{2,3,1,0:T(8,128)(2,1)} %copy.47, bf16[1,4,512,64]{2,3,1,0:T(8,128)(2,1)S(1)} %pad_maximum_fusion.1, s32[]{:T(128)} %constant.50.clone.1, s32[]{:T(128)} %constant.50.clone.1, s32[]{:T(128)S(6)} %select_n.58, s32[]{:T(128)} %constant.50.clone.1) | dynamic-update-slice | bytes 524292 | tf_op jit(solution)/shard_map/dynamic_update_slice | solution.py:220
  133.7 11.0 %collective-permute-done.3 = bf16[512,768]{1,0:T(8,128)(2,1)} collective-permute-done((bf16[512,768]{1,0:T(8,128)(2,1)}, bf16[512,768]{1,0:T(8,128)(2,1)}, u32[]{:S(2)}, u32[]{:S(2)}) %collective-permute-start.3) | collective-permute-done | bytes 786464 | tf_op jit(solution)/shard_map/ppermute | solution.py:145
  144.7 4.0 %fusion.25 = bf16[1,512,768]{2,1,0:T(8,128)(2,1)} fusion(bf16[512,768]{1,0:T(8,128)(2,1)} %collective-permute-done.3, f32[512,1536]{1,0:T(8,128)} %copy-done.4, s32[]{:T(128)S(6)} %select_n.53, bf16[2,192,512]{2,1,0:T(8,128)(2,1)S(1)} %copy-done.31, bf16[2,512,1536]{2,1,0:T(8,128)(2,1)} %all-gather.3.cloned.1.call-done, ...), kind=kOutput, calls=%fused_computation.32 | convolution fusion | flops 607322112 | bytes 5119488 | tf_op jit(solution)/shard_map/ect,ecd->td/dot_general | solution.py:273
  (67 shorter events, 0.2 us)
Async XLA Ops:
  7.2 59.2 %copy-start = (bf16[768,1536]{1,0:T(8,128)(2,1)S(1)}, bf16[768,1536]{1,0:T(8,128)(2,1)}, u32[]{:S(2)}) copy-start(bf16[768,1536]{1,0:T(8,128)(2,1)} %param.28) | copy-start | bytes 7077892
  7.2 105.9 %all-gather.5.cloned.1.call-start = ((), (), s32[]{:S(2)}) async-start(), calls=%async_computation.1 | async-start | bytes 6684672 | tf_op jit(solution)/shard_map/all_gather | solution.py:196
  7.2 2.6 %copy-start.5 = (bf16[1,4,2560,64]{2,3,1,0:T(8,128)(2,1)S(1)}, bf16[1,4,2560,64]{2,3,1,0:T(8,128)(2,1)}, u32[]{:S(2)}) copy-start(bf16[1,4,2560,64]{2,3,1,0:T(8,128)(2,1)} %param.18) | copy-start | bytes 3932164
  9.9 1.1 copy-start.12
  9.9 1.3 copy-start.13
  9.9 2.2 %copy-start.10 = (bf16[1,512,768]{2,1,0:T(8,128)(2,1)S(1)}, bf16[1,512,768]{2,1,0:T(8,128)(2,1)}, u32[]{:S(2)}) copy-start(bf16[1,512,768]{2,1,0:T(8,128)(2,1)} %param.16) | copy-start | bytes 2359300
  9.9 3.8 %copy-start.29 = (s32[16]{0:T(128)S(1)}, s32[16]{0:T(128)}, u32[]{:S(2)}) copy-start(s32[16]{0:T(128)} %param.19) | copy-start | bytes 196
  9.9 4.5 %copy-start.30 = (s32[16]{0:T(128)S(1)}, s32[16]{0:T(128)}, u32[]{:S(2)}) copy-start(s32[16]{0:T(128)} %param.20) | copy-start | bytes 196
  9.9 6.5 %copy-start.14 = (s32[1,512,8]{1,2,0:T(8,128)S(1)}, s32[1,512,8]{1,2,0:T(8,128)}, u32[]{:S(2)}) copy-start(s32[1,512,8]{1,2,0:T(8,128)} %param.21) | copy-start | bytes 49156
  12.0 109.3 %all-gather.3.cloned.1.call-start = ((), (), s32[]{:S(2)}) async-start(), calls=%async_computation | async-start | bytes 3342336 | tf_op jit(solution)/shard_map/all_gather | solution.py:199
  12.0 19.5 %collective-permute-start = (bf16[512,768]{1,0:T(8,128)(2,1)S(1)}, bf16[512,768]{1,0:T(8,128)(2,1)}, u32[]{:S(2)}, u32[]{:S(2)}) collective-permute-start(bf16[512,768]{1,0:T(8,128)(2,1)S(1)} %bitcast.92), channel_id=1, source_target_pairs={{0,1},{1,0},{2,3},{3,2},{4,5},{5,4},{6,7},{7,6},{8,9},{9,8},{10,11... | collective-permute-start | bytes 2359304 | tf_op jit(solution)/shard_map/ppermute | solution.py:145
  13.7 2.8 %copy-start.23 = (s32[2]{0:T(128)}, s32[2]{0:T(128)S(1)}, u32[]{:S(2)}) copy-start(s32[2]{0:T(128)S(1)} %iota_add_fusion) | copy-start | bytes 28
  16.5 0.6 copy-start.15
  19.3 13.8 %copy-start.26 = (bf16[1536,256]{1,0:T(8,128)(2,1)S(1)}, bf16[1536,256]{1,0:T(8,128)(2,1)}, u32[]{:S(2)}) copy-start(bf16[1536,256]{1,0:T(8,128)(2,1)} %param.26) | copy-start | bytes 2359300
  19.3 13.8 %copy-start.28 = (f32[1536]{0:T(1024)S(1)}, f32[1536]{0:T(1024)}, u32[]{:S(2)}) copy-start(f32[1536]{0:T(1024)} %param.23) | copy-start | bytes 18436
  32.7 1.2 copy-start.1
  33.1 1.8 %copy-start.25 = (bf16[1536,768]{1,0:T(8,128)(2,1)S(1)}, bf16[1536,768]{1,0:T(8,128)(2,1)}, u32[]{:S(2)}) copy-start(bf16[1536,768]{1,0:T(8,128)(2,1)} %param.25) | copy-start | bytes 7077892
  36.6 3.3 %copy-start.6 = (bf16[4,512,32]{1,2,0:T(8,128)(2,1)}, bf16[4,512,32]{1,2,0:T(8,128)(2,1)S(1)}, u32[]{:S(2)}) copy-start(bf16[4,512,32]{1,2,0:T(8,128)(2,1)S(1)} %get-tuple-element.21) | copy-start | bytes 393220
  36.6 3.3 %copy-start.8 = (bf16[4,512,32]{1,2,0:T(8,128)(2,1)}, bf16[4,512,32]{1,2,0:T(8,128)(2,1)S(1)}, u32[]{:S(2)}) copy-start(bf16[4,512,32]{1,2,0:T(8,128)(2,1)S(1)} %get-tuple-element.22) | copy-start | bytes 393220
  43.5 2.0 %copy-start.2 = (bf16[512,1536]{1,0:T(8,128)(2,1)S(1)}, bf16[512,1536]{1,0:T(8,128)(2,1)}, u32[]{:S(2)}) copy-start(bf16[512,1536]{1,0:T(8,128)(2,1)} %copy-done.1) | copy-start | bytes 4718596
  43.5 2.2 %copy-start.27 = (bf16[1536,256]{1,0:T(8,128)(2,1)S(1)}, bf16[1536,256]{1,0:T(8,128)(2,1)}, u32[]{:S(2)}) copy-start(bf16[1536,256]{1,0:T(8,128)(2,1)} %param.27) | copy-start | bytes 2359300
  66.4 2.4 %copy-start.16 = (s32[512,2]{0,1:T(2,128)S(1)}, s32[512,2]{0,1:T(2,128)}, u32[]{:S(2)}) copy-start(s32[512,2]{0,1:T(2,128)} %copy-done.15) | copy-start | bytes 12292
  67.2 24.9 %collective-permute-start.1 = (bf16[256,1536]{1,0:T(8,128)(2,1)S(1)}, bf16[256,1536]{1,0:T(8,128)(2,1)}, u32[]{:S(2)}, u32[]{:S(2)}) collective-permute-start(bf16[256,1536]{1,0:T(8,128)(2,1)S(1)} %convolution_convert_fusion.2), channel_id=1, source_target_pairs={{0,1},{1,0},{2,3},{3,2},{4,5},{5,4},{6,7},{7,6},{8,9},{9,8},{10,11... | collective-permute-start | bytes 2359304 | tf_op jit(solution)/shard_map/ppermute | solution.py:145
  90.3 1.4 copy-start.21
  90.3 1.4 copy-start.24
  90.4 1.5 copy-start.17
  90.4 1.5 copy-start.19
  91.2 18.5 %collective-permute-start.2 = (bf16[256,1536]{1,0:T(8,128)(2,1)S(1)}, bf16[256,1536]{1,0:T(8,128)(2,1)S(1)}, u32[]{:S(2)}, u32[]{:S(2)}) collective-permute-start(bf16[256,1536]{1,0:T(8,128)(2,1)S(1)} %convolution_convert_fusion.1), channel_id=1, source_target_pairs={{0,1},{1,0},{2,3},{3,2},{4,5},{5,4},{6,7},{7,6},{8,9},{9,8},{10,11... | collective-permute-start | bytes 2359304 | tf_op jit(solution)/shard_map/ppermute | solution.py:145
  93.4 16.5 %copy-start.3 = (bf16[512,1536]{1,0:T(8,128)(2,1)S(1)}, bf16[512,1536]{1,0:T(8,128)(2,1)}, u32[]{:S(2)}) copy-start(bf16[512,1536]{1,0:T(8,128)(2,1)} %copy-done.1) | copy-start | bytes 4718596
  109.9 2.2 %copy-start.22 = (f32[1536]{0:T(1024)S(1)}, f32[1536]{0:T(1024)}, u32[]{:S(2)}) copy-start(f32[1536]{0:T(1024)} %param.24) | copy-start | bytes 18436
  110.4 1.7 %copy-start.4 = (f32[512,1536]{1,0:T(8,128)}, f32[512,1536]{1,0:T(8,128)S(1)}, u32[]{:S(2)}) copy-start(f32[512,1536]{1,0:T(8,128)S(1)} %get-tuple-element.14) | copy-start | bytes 9437188
  117.2 4.0 %copy-start.18 = (s32[1,2,4,128]{3,1,2,0:T(2,128)S(1)}, s32[1,2,4,128]{3,1,2,0:T(2,128)}, u32[]{:S(2)}) copy-start(s32[1,2,4,128]{3,1,2,0:T(2,128)} %copy.40) | copy-start | bytes 12292
  117.2 4.0 %copy-start.20 = (pred[2,512]{1,0:T(4,128)(4,1)S(1)}, pred[2,512]{1,0:T(4,128)(4,1)}, u32[]{:S(2)}) copy-start(pred[2,512]{1,0:T(4,128)(4,1)} %broadcast_compare_fusion) | copy-start | bytes 3076
  118.8 9.3 %copy-start.11 = (bf16[512,256]{0,1:T(8,128)(2,1)S(1)}, bf16[512,256]{0,1:T(8,128)(2,1)}, u32[]{:S(2)}) copy-start(bf16[512,256]{0,1:T(8,128)(2,1)} %convolution_convert_fusion.3) | copy-start | bytes 786436
  118.8 12.1 %copy-start.7 = (bf16[4,512,32]{1,2,0:T(8,128)(2,1)S(1)}, bf16[4,512,32]{1,2,0:T(8,128)(2,1)}, u32[]{:S(2)}) copy-start(bf16[4,512,32]{1,2,0:T(8,128)(2,1)} %copy-done.6) | copy-start | bytes 393220
  118.8 12.1 %copy-start.9 = (bf16[4,512,32]{1,2,0:T(8,128)(2,1)S(1)}, bf16[4,512,32]{1,2,0:T(8,128)(2,1)}, u32[]{:S(2)}) copy-start(bf16[4,512,32]{1,2,0:T(8,128)(2,1)} %copy-done.8) | copy-start | bytes 393220
  124.7 20.0 %copy-start.31 = (bf16[2,192,512]{2,1,0:T(8,128)(2,1)S(1)}, bf16[2,192,512]{2,1,0:T(8,128)(2,1)}, u32[]{:S(2)}) copy-start(bf16[2,192,512]{2,1,0:T(8,128)(2,1)} %fusion.28) | copy-start | bytes 1179652
  124.7 20.0 %collective-permute-start.3 = (bf16[512,768]{1,0:T(8,128)(2,1)}, bf16[512,768]{1,0:T(8,128)(2,1)}, u32[]{:S(2)}, u32[]{:S(2)}) collective-permute-start(bf16[512,768]{1,0:T(8,128)(2,1)} %bitcast_convert_fusion), channel_id=1, source_target_pairs={{0,1},{1,0},{2,3},{3,2},{4,5},{5,4},{6,7},{7,6},{8,9},{9,8},{10,11... | collective-permute-start | bytes 2359304 | tf_op jit(solution)/shard_map/ppermute | solution.py:145
Sparse Core Ops, SparseCore 0:
  12.1 62.5 all-gather.4
  76.9 44.2 all-gather.2
where the time goes:
time: 158 us; the launch traced here: 155 us
  waiting for transfers between devices  41.9 us (27%)
  Pallas kernels  36.1 us (23%)
  local copies, waits for them, and re-layouts  26.9 us (17%)
  between operations  16.6 us (11%)
  matrix products  16.1 us (10%)
  other arithmetic  12.6 us (8%)
  starting transfers between devices  5.24 us (3%)
    ppermute x4, waiting for transfers between devices, shifted(): lax.ppermute(values, 'ep', [(i, (i + shift) % devices) for i in range(dev...  39.4 us
    pallas_call x2, Pallas kernels, flash_attend(): pl.pallas_call(kernel, grid_spec=grid_spec, out_shape=jax.ShapeDtypeStruc...  36.1 us
    unnamed x67, local copies, waits for them, and re-layouts  9.43 us
    dot_general x2, matrix products, expert_block(): jnp.einsum('ect,ecd->td', table, contrib, preferred_element_type=jnp.floa...  7.38 us
    ppermute x4, starting transfers between devices, shifted(): lax.ppermute(values, 'ep', [(i, (i + shift) % devices) for i in range(dev...  5.16 us
    squeeze x1, local copies, waits for them, and re-layouts, on_device(): up_whole = gate_up[1]  3.36 us
  transfers between devices with their start and end apart: 6, of which 4 were waited for; matrix products, arithmetic and copies ran while one was open for 25% of the time, Pallas kernels for 23%

commit v1 on v0

--- a/solution.py
+++ b/solution.py
@@ -194,8 +194,6 @@
     capacity = 3 * new_rows // 8
     me = lax.axis_index("ep")
     gate_up = lax.all_gather(jnp.stack([expert_gate, expert_up]), "req", axis=2, tiled=True)
-    gate_whole = gate_up[0]
-    up_whole = gate_up[1]
     down_whole = lax.all_gather(expert_down, "req", axis=1, tiled=True)
     everyone = jnp.arange(request_order.shape[0], dtype=jnp.int32)
     request = jnp.sum(jnp.where(everyone == lax.axis_index("req"), request_order, 0))
@@ -259,10 +257,9 @@
     dispatched = jnp.einsum(
         "ect,td->ecd", table, ffn_normed, preferred_element_type=jnp.float32
     ).astype(jnp.bfloat16)
-    gate_whole, up_whole, dispatched = lax.optimization_barrier((gate_whole, up_whole, dispatched))
-    gate_act = jnp.einsum("ecd,edf->ecf", dispatched, gate_whole, preferred_element_type=jnp.float32)
-    up_act = jnp.einsum("ecd,edf->ecf", dispatched, up_whole, preferred_element_type=jnp.float32)
-    act = (jax.nn.silu(gate_act) * up_act).astype(jnp.bfloat16)
+    gate_up, dispatched = lax.optimization_barrier((gate_up, dispatched))
+    both = jnp.einsum("ecd,kedf->kecf", dispatched, gate_up, preferred_element_type=jnp.float32)
+    act = (jax.nn.silu(both[0]) * both[1]).astype(jnp.bfloat16)
     down_whole, act = lax.optimization_barrier((down_whole, act))
     devices = lax.axis_size("ep")
 

time: 158 us -> 158 us (level)
  matrix products: 16.1 us -> 19.6 us
  local copies, waits for them, and re-layouts: 26.9 us -> 23.8 us
  other arithmetic: 12.6 us -> 10.8 us
    squeeze x1 -> x0, local copies, waits for them, and re-layouts: 3.36 us -> none  [on_device(): up_whole = gate_up[1]]
    dot_general x2 -> x1, matrix products: 2.33 us -> 4.28 us  [on_device(): jnp.einsum('ecd,kedf->kecf', dispatched, gate_up, preferred_element_type=...]
    mul x1, other arithmetic: 2.85 us -> 0.97 us  [on_device(): rotate(query.reshape(new_rows, heads_local, head_dim).transpose(1, 0, 2),...]
    dot_general x1, matrix products: 0.79 us -> 2.52 us  [on_device(): key_new = jnp.dot(normed, w_key, preferred_element_type=jnp.float32)]
  transfers between devices with their start and end apart: 6 -> 6, of which waited for: 4 -> 4; matrix products, arithmetic and copies ran while one was open for 25% -> 24% of each run, Pallas kernels for 23% -> 23%
where the time goes in v1:
time: 158 us; the launch traced here: 155 us
  waiting for transfers between devices  43.4 us (27%)
  Pallas kernels  36 us (23%)
  local copies, waits for them, and re-layouts  23.8 us (15%)
  matrix products  19.6 us (12%)
  between operations  16.4 us (10%)
  other arithmetic  10.8 us (7%)
  starting transfers between devices  5.29 us (3%)
    ppermute x4, waiting for transfers between devices, shifted(): lax.ppermute(values, 'ep', [(i, (i + shift) % devices) for i in range(dev...  39.3 us
    pallas_call x2, Pallas kernels, flash_attend(): pl.pallas_call(kernel, grid_spec=grid_spec, out_shape=jax.ShapeDtypeStruc...  36 us
    unnamed x67, local copies, waits for them, and re-layouts  9.69 us
    dot_general x2, matrix products, expert_block(): jnp.einsum('ect,ecd->td', table, contrib, preferred_element_type=jnp.floa...  7.25 us
    ppermute x4, starting transfers between devices, shifted(): lax.ppermute(values, 'ep', [(i, (i + shift) % devices) for i in range(dev...  5.21 us
    dot_general x1, matrix products, on_device(): jnp.einsum('ecd,kedf->kecf', dispatched, gate_up, preferred_element_type=...  4.28 us
    all_gather x1, waiting for transfers between devices, on_device(): down_whole = lax.all_gather(expert_down, 'req', axis=1, tiled=True)  4 us
  transfers between devices with their start and end apart: 6, of which 4 were waited for; matrix products, arithmetic and copies ran while one was open for 24% of the time, Pallas kernels for 23%

profile of v1, /device:TPU:16, one launch (start us, length us, event | category | flops | bytes accessed | tf_op | source)
XLA Modules:
  0.0 155.3 jit_solution(14590684525411746627)
XLA Ops:
  7.2 0.0 all-gather.5.cloned.1.call-start
  7.2 2.6 %copy.60 = bf16[1,4,2560,64]{2,3,1,0:T(8,128)(2,1)} copy(bf16[1,4,2560,64]{2,3,1,0:T(8,128)(2,1)} %param.18) | data formatting | bytes 2621440
  9.9 1.1 copy.59
  11.0 0.2 copy-done.15
  11.2 0.8 pad_maximum_fusion
  12.0 0.0 all-gather.3.cloned.1.call-start
  12.0 1.6 %collective-permute-start = (bf16[512,768]{1,0:T(8,128)(2,1)S(1)}, bf16[512,768]{1,0:T(8,128)(2,1)}, u32[]{:S(2)}, u32[]{:S(2)}) collective-permute-start(bf16[512,768]{1,0:T(8,128)(2,1)S(1)} %bitcast.103), channel_id=1, source_target_pairs={{0,1},{1,0},{2,3},{3,2},{4,5},{5,4},{6,7},{7,6},{8,9},{9,8},{10,11... | collective-permute-start | bytes 2359304 | tf_op jit(solution)/shard_map/ppermute | solution.py:145
  13.7 0.6 fusion.56
  14.3 1.3 fusion.57
  15.6 0.6 add_convert_fusion.3
  16.3 0.1 fusion.50
  16.4 0.5 copy-done.25
  16.8 0.6 copy-done.17
  17.4 0.6 reduce-window.6
  18.0 0.2 slice_reduce_fusion
  18.3 0.2 reduce-window.9
  18.5 0.7 add_bitcast_fusion
  19.1 0.3 multiply_cosine_fusion
  19.4 0.1 broadcast_in_dim.33
  19.6 0.1 constant_dynamic-update-slice_fusion.1
  19.6 11.8 %collective-permute-done = bf16[512,768]{1,0:T(8,128)(2,1)} collective-permute-done((bf16[512,768]{1,0:T(8,128)(2,1)S(1)}, bf16[512,768]{1,0:T(8,128)(2,1)}, u32[]{:S(2)}, u32[]{:S(2)}) %collective-permute-start) | collective-permute-done | bytes 786464 | tf_op jit(solution)/shard_map/ppermute | solution.py:145
  31.5 1.2 constant_dynamic-update-slice_fusion
  32.7 0.4 fusion.2
  33.1 1.6 %fusion.61 = f32[512,768]{0,1:T(8,128)S(1)} fusion(bf16[1536,768]{1,0:T(8,128)(2,1)S(1)} %copy-done.27, bf16[512,1536]{1,0:T(8,128)(2,1)S(1)} %constant_dynamic-update-slice_fusion, f32[1536]{0:T(1024)S(1)} %copy-done.29, f32[512]{0:T(512)S(1)} %add_rsqrt_fusion.1), kind=kOutput, calls=%fused_computation.82 | convolution fusion | flops 1211105280 | bytes 5513216 | tf_op jit(solution)/shard_map/dot_general | solution.py:204
  34.7 0.3 subtract_convert_fusion
  34.9 1.5 copy.37
  36.5 1.5 copy.38
  38.0 2.5 %fusion.59 = f32[512,256]{0,1:T(8,128)S(1)} fusion(bf16[1536,256]{1,0:T(8,128)(2,1)} %param.26, bf16[512,1536]{1,0:T(8,128)(2,1)} %copy-done.1, f32[1536]{0:T(1024)S(1)} %copy-done.29, f32[512]{0:T(512)S(1)} %add_rsqrt_fusion.1), kind=kOutput, calls=%fused_computation.81 | convolution fusion | flops 405798912 | bytes 2891776 | tf_op jit(solution)/shard_map/dot_general | solution.py:205
  40.5 0.1 subtract_convert_fusion.1
  40.6 0.6 copy-done.8
  41.2 0.0 copy-done.10
  41.3 0.7 maximum_bitcast_fusion.kn_ref
  42.0 1.0 maximum_multiply_fusion
  43.0 1.2 fusion.64
  44.2 0.8 copy-done.2
  45.0 0.2 copy-done.28
  45.2 1.5 convolution_convert_fusion.3
  46.7 17.8 %shard_map.175 = bf16[4,768,64]{2,1,0:T(8,128)(2,1)} custom-call(s32[1]{0:T(128)} %bitcast.1.length_ref, bf16[4,768,64]{2,1,0:T(8,128)(2,1)} %bitcast.107, bf16[4,64,2560]{2,1,0:T(8,128)(2,1)} %bitcast.99, bf16[4,64,2560]{2,1,0:T(8,128)(2,1)} %bitcast.97, bf16[4,64,512]{2,1,0:T(8,128)(2,1)} %maximum_bitcast_fusion.kn_ref, bf16[4,64,512]{2,1,0:T(8,128)(2,1)} %bitcast.109), custom_call_target="tpu_custom_call" | custom-call | flops 2013265920 | bytes 3407872 | tf_op jit(solution)/shard_map/pallas_call | solution.py:130
  64.5 1.4 copy.39
  65.9 0.8 convolution_convert_fusion.2
  66.7 1.6 %collective-permute-start.1 = (bf16[256,1536]{1,0:T(8,128)(2,1)S(1)}, bf16[256,1536]{1,0:T(8,128)(2,1)}, u32[]{:S(2)}, u32[]{:S(2)}) collective-permute-start(bf16[256,1536]{1,0:T(8,128)(2,1)S(1)} %convolution_convert_fusion.2), channel_id=1, source_target_pairs={{0,1},{1,0},{2,3},{3,2},{4,5},{5,4},{6,7},{7,6},{8,9},{9,8},{10,11... | collective-permute-start | bytes 2359304 | tf_op jit(solution)/shard_map/ppermute | solution.py:145
  68.3 0.6 broadcast_compare_fusion
  68.9 1.3 copy.52
  70.2 18.2 %shard_map.176 = bf16[4,768,64]{2,1,0:T(8,128)(2,1)} custom-call(s32[1]{0:T(128)} %bitcast.1.length_ref, bf16[4,768,64]{2,1,0:T(8,128)(2,1)} %bitcast.106, bf16[4,64,2560]{2,1,0:T(8,128)(2,1)} %bitcast.100, bf16[4,64,2560]{2,1,0:T(8,128)(2,1)} %bitcast.98, bf16[4,64,512]{2,1,0:T(8,128)(2,1)} %maximum_bitcast_fusion.kn_ref, bf16[4,64,512]{2,1,0:T(8,128)(2,1)} %bitcast.110), custom_call_target="tpu_custom_call" | custom-call | flops 2013265920 | bytes 3407872 | tf_op jit(solution)/shard_map/pallas_call | solution.py:130
  88.4 1.4 copy.40
  89.8 0.8 convolution_convert_fusion.1
  90.6 0.6 collective-permute-start.2
  91.2 0.1 fusion.51
  91.3 0.2 select_reduce_fusion
  91.5 1.3 convert_add_fusion.2
  92.9 16.3 %collective-permute-done.2 = bf16[256,1536]{1,0:T(8,128)(2,1)S(1)} collective-permute-done((bf16[256,1536]{1,0:T(8,128)(2,1)S(1)}, bf16[256,1536]{1,0:T(8,128)(2,1)S(1)}, u32[]{:S(2)}, u32[]{:S(2)}) %collective-permute-start.2) | collective-permute-done | bytes 786464 | tf_op jit(solution)/shard_map/ppermute | solution.py:145
  109.3 0.2 convert_add_fusion.1
  109.5 0.5 multiply_reduce_fusion
  110.0 1.6 %copy-done.4 = f32[512,1536]{1,0:T(8,128)} copy-done((f32[512,1536]{1,0:T(8,128)}, f32[512,1536]{1,0:T(8,128)S(1)}, u32[]{:S(2)}) %copy-start.4) | copy-done | bytes 3145752
  111.6 1.0 convolution_convert_fusion
  112.7 4.3 %fusion.15 = f32[2,2,192,512]{3,2,0,1:T(8,128)S(1)} fusion(bf16[2,2,1536,512]{3,2,1,0:T(8,128)(2,1)} %all-gather.5.cloned.1.call-done, bf16[2,192,1536]{2,1,0:T(8,128)(2,1)S(1)} %convolution_convert_fusion), kind=kOutput, calls=%fused_computation.28 | convolution fusion | flops 1207959552 | bytes 9043968 | tf_op jit(solution)/shard_map/ecd,kedf->kecf/dot_general | solution.py:261
  117.0 0.2 fusion.37
  117.2 4.0 %all-gather.3.cloned.1.call-done = bf16[2,512,1536]{2,1,0:T(8,128)(2,1)} async-done(((bf16[2,32,1536]{2,1,0:T(8,128)(2,1)}), bf16[2,512,1536]{2,1,0:T(8,128)(2,1)}) %all-gather.3.cloned.1.call-update) | async-done | bytes 3145744 | tf_op jit(solution)/shard_map/all_gather | solution.py:197
  121.2 3.3 %bitcast_convert_fusion = bf16[512,768]{1,0:T(8,128)(2,1)} fusion(bf16[2,192,512]{2,1,0:T(8,128)(2,1)S(1)} %fusion.37, bf16[2,512,1536]{2,1,0:T(8,128)(2,1)} %all-gather.3.cloned.1.call-done, s32[]{:T(128)S(6)} %select_n.57, f32[2,192]{1,0:T(2,128)S(1)} %select_reduce_fusion, s32[2,512]{1,0:T(2,128)S(1)} %bitcast.119, pred[2,512]{1,0:T(4,128)(4,1)S(1)} %copy-done.22), kind=kOutput, calls=%fused_computation.17 | convolution fusion | flops 605356032 | bytes 2759172 | tf_op jit(solution)/shard_map/ect,ecd->td/dot_general | solution.py:270
  124.5 1.5 collective-permute-start.3
  127.9 2.8 %dynamic_update_slice.16 = bf16[1,4,2560,64]{2,3,1,0:T(8,128)(2,1)} dynamic-update-slice(bf16[1,4,2560,64]{2,3,1,0:T(8,128)(2,1)} %copy.59, bf16[1,4,512,64]{2,3,1,0:T(8,128)(2,1)S(1)} %pad_maximum_fusion.1, s32[]{:T(128)} %constant.50.clone.1, s32[]{:T(128)} %constant.50.clone.1, s32[]{:T(128)S(6)} %select_n.58, s32[]{:T(128)} %constant.50.clone.1) | dynamic-update-slice | bytes 524292 | tf_op jit(solution)/shard_map/dynamic_update_slice | solution.py:218
  130.6 2.7 %dynamic_update_slice.17 = bf16[1,4,2560,64]{2,3,1,0:T(8,128)(2,1)} dynamic-update-slice(bf16[1,4,2560,64]{2,3,1,0:T(8,128)(2,1)} %copy.60, bf16[1,4,512,64]{2,3,1,0:T(8,128)(2,1)S(1)} %bitcast.111, s32[]{:T(128)} %constant.50.clone.1, s32[]{:T(128)} %constant.50.clone.1, s32[]{:T(128)S(6)} %select_n.58, s32[]{:T(128)} %constant.50.clone.1) | dynamic-update-slice | bytes 524292 | tf_op jit(solution)/shard_map/dynamic_update_slice | solution.py:219
  133.4 11.2 %collective-permute-done.3 = bf16[512,768]{1,0:T(8,128)(2,1)} collective-permute-done((bf16[512,768]{1,0:T(8,128)(2,1)}, bf16[512,768]{1,0:T(8,128)(2,1)}, u32[]{:S(2)}, u32[]{:S(2)}) %collective-permute-start.3) | collective-permute-done | bytes 786464 | tf_op jit(solution)/shard_map/ppermute | solution.py:145
  144.5 4.0 %fusion.30 = bf16[1,512,768]{2,1,0:T(8,128)(2,1)} fusion(bf16[512,768]{1,0:T(8,128)(2,1)} %collective-permute-done.3, f32[512,1536]{1,0:T(8,128)} %copy-done.4, s32[]{:T(128)S(6)} %select_n.53, bf16[2,192,512]{2,1,0:T(8,128)(2,1)S(1)} %fusion.37, bf16[2,512,1536]{2,1,0:T(8,128)(2,1)} %all-gather.3.cloned.1.call-done, f32[2,192]{1,0:T(2,128)S(1)} %select_reduce_fusion, ...), kind=kOutput, calls=%fused_computation.33 | convolution fusion | flops 607322112 | bytes 5119488 | tf_op jit(solution)/shard_map/ect,ecd->td/dot_general | solution.py:270
  (66 shorter events, 0.3 us)
Async XLA Ops:
  7.2 58.8 %copy-start = (bf16[768,1536]{1,0:T(8,128)(2,1)S(1)}, bf16[768,1536]{1,0:T(8,128)(2,1)}, u32[]{:S(2)}) copy-start(bf16[768,1536]{1,0:T(8,128)(2,1)} %param.28) | copy-start | bytes 7077892
  7.2 105.5 %all-gather.5.cloned.1.call-start = ((), (), s32[]{:S(2)}) async-start(), calls=%async_computation.1 | async-start | bytes 6684672 | tf_op jit(solution)/shard_map/all_gather | solution.py:196
  7.2 2.6 %copy-start.7 = (bf16[1,4,2560,64]{2,3,1,0:T(8,128)(2,1)S(1)}, bf16[1,4,2560,64]{2,3,1,0:T(8,128)(2,1)}, u32[]{:S(2)}) copy-start(bf16[1,4,2560,64]{2,3,1,0:T(8,128)(2,1)} %param.17) | copy-start | bytes 3932164
  9.9 1.1 copy-start.14
  9.9 1.3 copy-start.15
  9.9 2.2 %copy-start.12 = (bf16[1,512,768]{2,1,0:T(8,128)(2,1)S(1)}, bf16[1,512,768]{2,1,0:T(8,128)(2,1)}, u32[]{:S(2)}) copy-start(bf16[1,512,768]{2,1,0:T(8,128)(2,1)} %param.16) | copy-start | bytes 2359300
  9.9 3.8 %copy-start.30 = (s32[16]{0:T(128)S(1)}, s32[16]{0:T(128)}, u32[]{:S(2)}) copy-start(s32[16]{0:T(128)} %param.19) | copy-start | bytes 196
  9.9 4.4 %copy-start.31 = (s32[16]{0:T(128)S(1)}, s32[16]{0:T(128)}, u32[]{:S(2)}) copy-start(s32[16]{0:T(128)} %param.20) | copy-start | bytes 196
  9.9 6.4 %copy-start.16 = (s32[1,512,8]{1,2,0:T(8,128)S(1)}, s32[1,512,8]{1,2,0:T(8,128)}, u32[]{:S(2)}) copy-start(s32[1,512,8]{1,2,0:T(8,128)} %param.21) | copy-start | bytes 49156
  12.0 109.3 %all-gather.3.cloned.1.call-start = ((), (), s32[]{:S(2)}) async-start(), calls=%async_computation | async-start | bytes 3342336 | tf_op jit(solution)/shard_map/all_gather | solution.py:197
  12.0 19.5 %collective-permute-start = (bf16[512,768]{1,0:T(8,128)(2,1)S(1)}, bf16[512,768]{1,0:T(8,128)(2,1)}, u32[]{:S(2)}, u32[]{:S(2)}) collective-permute-start(bf16[512,768]{1,0:T(8,128)(2,1)S(1)} %bitcast.103), channel_id=1, source_target_pairs={{0,1},{1,0},{2,3},{3,2},{4,5},{5,4},{6,7},{7,6},{8,9},{9,8},{10,11... | collective-permute-start | bytes 2359304 | tf_op jit(solution)/shard_map/ppermute | solution.py:145
  16.3 0.6 copy-start.25
  16.8 0.6 copy-start.17
  19.6 13.5 %copy-start.27 = (bf16[1536,768]{1,0:T(8,128)(2,1)S(1)}, bf16[1536,768]{1,0:T(8,128)(2,1)}, u32[]{:S(2)}) copy-start(bf16[1536,768]{1,0:T(8,128)(2,1)} %param.25) | copy-start | bytes 7077892
  19.6 13.5 %copy-start.29 = (f32[1536]{0:T(1024)S(1)}, f32[1536]{0:T(1024)}, u32[]{:S(2)}) copy-start(f32[1536]{0:T(1024)} %param.23) | copy-start | bytes 18436
  32.7 2.0 %copy-start.1 = (bf16[512,1536]{1,0:T(8,128)(2,1)}, bf16[512,1536]{1,0:T(8,128)(2,1)S(1)}, u32[]{:S(2)}) copy-start(bf16[512,1536]{1,0:T(8,128)(2,1)S(1)} %constant_dynamic-update-slice_fusion) | copy-start | bytes 4718596
  37.9 4.0 %copy-start.5 = (bf16[4,3,512,32]{3,2,1,0:T(8,128)(2,1)S(1)}, bf16[4,3,512,32]{3,2,1,0:T(8,128)(2,1)}, u32[]{:S(2)}) copy-start(bf16[4,3,512,32]{3,2,1,0:T(8,128)(2,1)} %copy.37) | copy-start | bytes 1179652
  38.0 4.1 %copy-start.6 = (bf16[4,3,512,32]{3,2,1,0:T(8,128)(2,1)S(1)}, bf16[4,3,512,32]{3,2,1,0:T(8,128)(2,1)}, u32[]{:S(2)}) copy-start(bf16[4,3,512,32]{3,2,1,0:T(8,128)(2,1)} %copy.38) | copy-start | bytes 1179652
  40.6 0.7 copy-start.8
  40.6 0.7 copy-start.10
  43.0 2.1 %copy-start.2 = (bf16[512,1536]{1,0:T(8,128)(2,1)S(1)}, bf16[512,1536]{1,0:T(8,128)(2,1)}, u32[]{:S(2)}) copy-start(bf16[512,1536]{1,0:T(8,128)(2,1)} %copy-done.1) | copy-start | bytes 4718596
  43.0 2.3 %copy-start.28 = (bf16[1536,256]{1,0:T(8,128)(2,1)S(1)}, bf16[1536,256]{1,0:T(8,128)(2,1)}, u32[]{:S(2)}) copy-start(bf16[1536,256]{1,0:T(8,128)(2,1)} %param.27) | copy-start | bytes 2359300
  65.9 2.4 %copy-start.18 = (s32[512,2]{0,1:T(2,128)S(1)}, s32[512,2]{0,1:T(2,128)}, u32[]{:S(2)}) copy-start(s32[512,2]{0,1:T(2,128)} %copy-done.17) | copy-start | bytes 12292
  66.7 24.8 %collective-permute-start.1 = (bf16[256,1536]{1,0:T(8,128)(2,1)S(1)}, bf16[256,1536]{1,0:T(8,128)(2,1)}, u32[]{:S(2)}, u32[]{:S(2)}) collective-permute-start(bf16[256,1536]{1,0:T(8,128)(2,1)S(1)} %convolution_convert_fusion.2), channel_id=1, source_target_pairs={{0,1},{1,0},{2,3},{3,2},{4,5},{5,4},{6,7},{7,6},{8,9},{9,8},{10,11... | collective-permute-start | bytes 2359304 | tf_op jit(solution)/shard_map/ppermute | solution.py:145
  89.8 1.4 copy-start.23
  89.8 1.4 copy-start.26
  89.8 1.5 copy-start.19
  89.8 1.5 copy-start.21
  90.6 18.7 %collective-permute-start.2 = (bf16[256,1536]{1,0:T(8,128)(2,1)S(1)}, bf16[256,1536]{1,0:T(8,128)(2,1)S(1)}, u32[]{:S(2)}, u32[]{:S(2)}) collective-permute-start(bf16[256,1536]{1,0:T(8,128)(2,1)S(1)} %convolution_convert_fusion.1), channel_id=1, source_target_pairs={{0,1},{1,0},{2,3},{3,2},{4,5},{5,4},{6,7},{7,6},{8,9},{9,8},{10,11... | collective-permute-start | bytes 2359304 | tf_op jit(solution)/shard_map/ppermute | solution.py:145
  92.9 16.6 %copy-start.3 = (bf16[512,1536]{1,0:T(8,128)(2,1)S(1)}, bf16[512,1536]{1,0:T(8,128)(2,1)}, u32[]{:S(2)}) copy-start(bf16[512,1536]{1,0:T(8,128)(2,1)} %copy-done.1) | copy-start | bytes 4718596
  109.5 2.2 %copy-start.24 = (f32[1536]{0:T(1024)S(1)}, f32[1536]{0:T(1024)}, u32[]{:S(2)}) copy-start(f32[1536]{0:T(1024)} %param.24) | copy-start | bytes 18436
  110.0 1.7 %copy-start.4 = (f32[512,1536]{1,0:T(8,128)}, f32[512,1536]{1,0:T(8,128)S(1)}, u32[]{:S(2)}) copy-start(f32[512,1536]{1,0:T(8,128)S(1)} %get-tuple-element.12) | copy-start | bytes 9437188
  116.9 4.3 %copy-start.20 = (s32[1,2,4,128]{3,1,2,0:T(2,128)S(1)}, s32[1,2,4,128]{3,1,2,0:T(2,128)}, u32[]{:S(2)}) copy-start(s32[1,2,4,128]{3,1,2,0:T(2,128)} %copy.52) | copy-start | bytes 12292
  116.9 4.3 %copy-start.22 = (pred[2,512]{1,0:T(4,128)(4,1)S(1)}, pred[2,512]{1,0:T(4,128)(4,1)}, u32[]{:S(2)}) copy-start(pred[2,512]{1,0:T(4,128)(4,1)} %broadcast_compare_fusion) | copy-start | bytes 3076
  117.2 10.6 %copy-start.9 = (bf16[4,512,32]{1,2,0:T(8,128)(2,1)S(1)}, bf16[4,512,32]{1,2,0:T(8,128)(2,1)}, u32[]{:S(2)}) copy-start(bf16[4,512,32]{1,2,0:T(8,128)(2,1)} %copy-done.8) | copy-start | bytes 393220
  117.2 10.6 %copy-start.11 = (bf16[4,512,32]{1,2,0:T(8,128)(2,1)S(1)}, bf16[4,512,32]{1,2,0:T(8,128)(2,1)}, u32[]{:S(2)}) copy-start(bf16[4,512,32]{1,2,0:T(8,128)(2,1)} %copy-done.10) | copy-start | bytes 393220
  117.2 13.4 %copy-start.13 = (bf16[512,256]{0,1:T(8,128)(2,1)S(1)}, bf16[512,256]{0,1:T(8,128)(2,1)}, u32[]{:S(2)}) copy-start(bf16[512,256]{0,1:T(8,128)(2,1)} %convolution_convert_fusion.3) | copy-start | bytes 786436
  124.5 20.0 %collective-permute-start.3 = (bf16[512,768]{1,0:T(8,128)(2,1)}, bf16[512,768]{1,0:T(8,128)(2,1)}, u32[]{:S(2)}, u32[]{:S(2)}) collective-permute-start(bf16[512,768]{1,0:T(8,128)(2,1)} %bitcast_convert_fusion), channel_id=1, source_target_pairs={{0,1},{1,0},{2,3},{3,2},{4,5},{5,4},{6,7},{7,6},{8,9},{9,8},{10,11... | collective-permute-start | bytes 2359304 | tf_op jit(solution)/shard_map/ppermute | solution.py:145
Sparse Core Ops, SparseCore 0:
  12.1 62.5 all-gather.4
  77.0 44.2 all-gather.2

commit v2 on v1

--- a/solution.py
+++ b/solution.py
@@ -193,8 +193,20 @@
     per_device = expert_gate.shape[0]
     capacity = 3 * new_rows // 8
     me = lax.axis_index("ep")
-    gate_up = lax.all_gather(jnp.stack([expert_gate, expert_up]), "req", axis=2, tiled=True)
-    down_whole = lax.all_gather(expert_down, "req", axis=1, tiled=True)
+    req_devices = lax.axis_size("req")
+    down_rows = expert_down.shape[1]
+    weights = lax.all_gather(
+        jnp.stack([expert_gate, expert_up, expert_down.reshape(expert_gate.shape)]),
+        "req",
+        axis=2,
+        tiled=True,
+    )
+    gate_up = weights[:2]
+    down_whole = (
+        weights[2]
+        .reshape((per_device, req_devices) + expert_gate.shape[1:])
+        .reshape(per_device, req_devices * down_rows, expert_down.shape[2])
+    )
     everyone = jnp.arange(request_order.shape[0], dtype=jnp.int32)
     request = jnp.sum(jnp.where(everyone == lax.axis_index("req"), request_order, 0))
     length = jnp.sum(jnp.where(everyone == request, cached_lengths, 0))

time: 158 us -> 166 us (1.051)
  local copies, waits for them, and re-layouts: 23.8 us -> 39.5 us
  waiting for transfers between devices: 43.4 us -> 34.3 us
  Pallas kernels: 36 us -> 39.6 us
  matrix products: 19.6 us -> 16.8 us
  other arithmetic: 10.8 us -> 13.1 us
    another operation x0 -> x2, local copies, waits for them, and re-layouts: none -> 6.96 us  [the longest x1 5.87 us: on_device(): down_whole = weights[2].reshape((per_device, req_devices) + expert_gate.s...]
    slice x1 -> x4, local copies, waits for them, and re-layouts: 0.21 us -> 6.73 us  [the longest x1 3.73 us: on_device(): weights[2].reshape((per_device, req_devices) + expert_gate.shape[1:])]
    ppermute x4, waiting for transfers between devices: 39.3 us -> 34.3 us  [shifted(): lax.ppermute(values, 'ep', [(i, (i + shift) % devices) for i in range(dev...]
    all_gather x2 -> x1, waiting for transfers between devices: 4.02 us -> 0.02 us  [on_device(): lax.all_gather(jnp.stack([expert_gate, expert_up, expert_down.reshape(exp...]
    pallas_call x2, Pallas kernels: 36 us -> 39.6 us  [flash_attend(): pl.pallas_call(kernel, grid_spec=grid_spec, out_shape=jax.ShapeDtypeStruc...]
    dot_general x1, matrix products: 4.28 us -> 1.38 us  [on_device(): jnp.einsum('ecd,kedf->kecf', dispatched, gate_up, preferred_element_type=...]
    unnamed x67 -> x61, local copies, waits for them, and re-layouts: 9.69 us -> 9.79 us
  transfers between devices with their start and end apart: 6 -> 5, of which waited for: 4 -> 3; matrix products, arithmetic and copies ran while one was open for 24% -> 22% of each run, Pallas kernels for 23% -> 24%
where the time goes in v2:
time: 166 us; the launch traced here: 164 us
  Pallas kernels  39.6 us (24%)
  local copies, waits for them, and re-layouts  39.5 us (24%)
  waiting for transfers between devices  34.3 us (21%)
  matrix products  16.8 us (10%)
  between operations  16.1 us (10%)
  other arithmetic  13.1 us (8%)
  starting transfers between devices  4.3 us (3%)
    pallas_call x2, Pallas kernels, flash_attend(): pl.pallas_call(kernel, grid_spec=grid_spec, out_shape=jax.ShapeDtypeStruc...  39.6 us
    ppermute x4, waiting for transfers between devices, shifted(): lax.ppermute(values, 'ep', [(i, (i + shift) % devices) for i in range(dev...  34.3 us
    unnamed x61, local copies, waits for them, and re-layouts  9.79 us
    dot_general x2, matrix products, expert_block(): jnp.einsum('ect,ecd->td', table, contrib, preferred_element_type=jnp.floa...  7.31 us
    another operation x1, local copies, waits for them, and re-layouts, on_device(): down_whole = weights[2].reshape((per_device, req_devices) + expert_gate.s...  5.87 us
    ppermute x4, starting transfers between devices, shifted(): lax.ppermute(values, 'ep', [(i, (i + shift) % devices) for i in range(dev...  4.27 us
    dynamic_update_slice x1, local copies, waits for them, and re-layouts, on_device(): keys = lax.dynamic_update_slice(key_cache[0], key_new, (zero, length, zero))  3.8 us
    dynamic_update_slice x1, local copies, waits for them, and re-layouts, on_device(): lax.dynamic_update_slice(value_cache[0], value_new, (zero, length, zero))  3.78 us
  transfers between devices with their start and end apart: 5, of which 3 were waited for; matrix products, arithmetic and copies ran while one was open for 22% of the time, Pallas kernels for 24%

profile of v2, /device:TPU:16, one launch (start us, length us, event | category | flops | bytes accessed | tf_op | source)
XLA Modules:
  0.0 163.7 jit_solution(4406973632175405145)
XLA Ops:
  7.2 2.6 %copy.59 = bf16[1,4,2560,64]{2,3,1,0:T(8,128)(2,1)} copy(bf16[1,4,2560,64]{2,3,1,0:T(8,128)(2,1)} %param.17) | data formatting | bytes 2621440
  9.9 1.1 copy.60
  10.9 1.1 stack_reshape.3
  12.0 1.8 %pad_maximum_fusion = bf16[3,2,96,512]{3,2,1,0:T(8,128)(2,1)} fusion(bf16[1,2,96,512]{3,2,1,0:T(8,128)(2,1)S(1)} %stack_reshape.3, bf16[1,2,96,512]{3,2,1,0:T(8,128)(2,1)S(1)} %bitcast.114, bf16[1,2,96,512]{3,2,1,0:T(8,128)(2,1)} %bitcast.115), kind=kLoop, calls=%fused_computation.45 | loop fusion | flops 589824 | bytes 1179648 | tf_op jit(solution)/shard_map/stack | solution.py:199
  13.9 1.6 collective-permute-start
  15.5 0.1 fusion.50
  15.6 0.5 copy-done.24
  16.0 0.6 copy-done.16
  16.6 0.6 reduce-window.6
  17.2 0.2 slice_reduce_fusion
  17.5 0.2 reduce-window.9
  17.6 1.3 fusion.56
  18.9 1.9 %fusion.57 = s32[]{:T(128)} fusion(s32[16]{0:T(128)} %param.20, s32[]{:T(128)} %fusion.56), kind=kLoop, calls=%fused_computation.78 | loop fusion | flops 47 | bytes 72 | tf_op jit(solution)/shard_map/reduce_sum | solution.py:212
  20.9 0.6 add_convert_fusion.3
  21.5 0.7 add_bitcast_fusion
  22.1 0.3 multiply_cosine_fusion
  22.4 0.1 broadcast_in_dim.33
  22.5 0.1 constant_dynamic-update-slice_fusion.1
  22.6 10.7 %collective-permute-done = bf16[512,768]{1,0:T(8,128)(2,1)} collective-permute-done((bf16[512,768]{1,0:T(8,128)(2,1)S(1)}, bf16[512,768]{1,0:T(8,128)(2,1)}, u32[]{:S(2)}, u32[]{:S(2)}) %collective-permute-start) | collective-permute-done | bytes 786464 | tf_op jit(solution)/shard_map/ppermute | solution.py:145
  33.3 1.2 constant_dynamic-update-slice_fusion
  34.6 0.4 fusion.2
  35.0 1.6 fusion.61
  36.5 0.3 subtract_convert_fusion
  36.8 1.5 copy.38
  38.3 1.5 copy.37
  39.8 2.5 %fusion.59 = f32[512,256]{0,1:T(8,128)S(1)} fusion(bf16[1536,256]{1,0:T(8,128)(2,1)} %param.26, bf16[512,1536]{1,0:T(8,128)(2,1)} %copy-done.1, f32[1536]{0:T(1024)S(1)} %copy-done.28, f32[512]{0:T(512)S(1)} %add_rsqrt_fusion.1), kind=kOutput, calls=%fused_computation.81 | convolution fusion | flops 405798912 | bytes 2891776 | tf_op jit(solution)/shard_map/dot_general | solution.py:217
  42.4 0.1 subtract_convert_fusion.1
  42.5 0.6 copy-done.8
  43.1 0.7 maximum_bitcast_fusion.kn_ref
  43.9 1.0 maximum_multiply_fusion
  44.9 1.2 fusion.64
  46.1 0.7 copy-done.2
  46.8 0.2 copy-done.27
  47.0 1.5 convolution_convert_fusion.3
  48.5 20.0 %shard_map.176 = bf16[4,768,64]{2,1,0:T(8,128)(2,1)} custom-call(s32[1]{0:T(128)} %bitcast.1.length_ref, bf16[4,768,64]{2,1,0:T(8,128)(2,1)} %bitcast.109, bf16[4,64,2560]{2,1,0:T(8,128)(2,1)} %bitcast.101, bf16[4,64,2560]{2,1,0:T(8,128)(2,1)} %bitcast.99, bf16[4,64,512]{2,1,0:T(8,128)(2,1)} %maximum_bitcast_fusion.kn_ref, bf16[4,64,512]{2,1,0:T(8,128)(2,1)} %bitcast.111), custom_call_target="tpu_custom_call" | custom-call | flops 2013265920 | bytes 3407872 | tf_op jit(solution)/shard_map/pallas_call | solution.py:130
  68.5 1.4 copy.40
  69.9 0.8 convolution_convert_fusion.1
  70.7 1.6 collective-permute-start.2
  72.3 0.6 broadcast_compare_fusion
  72.8 1.3 copy.52
  74.1 19.6 %shard_map.175 = bf16[4,768,64]{2,1,0:T(8,128)(2,1)} custom-call(s32[1]{0:T(128)} %bitcast.1.length_ref, bf16[4,768,64]{2,1,0:T(8,128)(2,1)} %bitcast.108, bf16[4,64,2560]{2,1,0:T(8,128)(2,1)} %bitcast.102, bf16[4,64,2560]{2,1,0:T(8,128)(2,1)} %bitcast.100, bf16[4,64,512]{2,1,0:T(8,128)(2,1)} %maximum_bitcast_fusion.kn_ref, bf16[4,64,512]{2,1,0:T(8,128)(2,1)} %bitcast.112), custom_call_target="tpu_custom_call" | custom-call | flops 2013265920 | bytes 3407872 | tf_op jit(solution)/shard_map/pallas_call | solution.py:130
  93.7 1.4 copy.39
  95.2 0.8 convolution_convert_fusion.2
  96.0 0.6 collective-permute-start.1
  96.6 0.1 fusion.51
  96.7 0.2 select_reduce_fusion
  96.9 1.3 convert_add_fusion.1
  98.3 15.9 %collective-permute-done.1 = bf16[256,1536]{1,0:T(8,128)(2,1)S(1)} collective-permute-done((bf16[256,1536]{1,0:T(8,128)(2,1)S(1)}, bf16[256,1536]{1,0:T(8,128)(2,1)S(1)}, u32[]{:S(2)}, u32[]{:S(2)}) %collective-permute-start.1) | collective-permute-done | bytes 786464 | tf_op jit(solution)/shard_map/ppermute | solution.py:145
  114.2 0.2 convert_add_fusion.2
  114.4 0.5 multiply_reduce_fusion
  114.9 1.6 %copy-done.4 = f32[512,1536]{1,0:T(8,128)} copy-done((f32[512,1536]{1,0:T(8,128)}, f32[512,1536]{1,0:T(8,128)S(1)}, u32[]{:S(2)}) %copy-start.4) | copy-done | bytes 3145752
  116.6 1.0 convolution_convert_fusion
  117.6 3.7 %slice.55 = bf16[1,2,1536,512]{3,2,1,0:T(8,128)(2,1)} slice(bf16[3,2,1536,512]{3,2,1,0:T(8,128)(2,1)} %all-gather.2.cloned.1.call-done), slice={[2:3], [0:2], [0:1536], [0:512]} | slice | bytes 6291456 | tf_op jit(solution)/shard_map/slice | solution.py:206
  121.3 5.9 %reshape_reshape_squeeze.3 = bf16[2,512,1536]{2,1,0:T(8,128)(2,1)} reshape(bf16[1,2,1536,512]{3,2,1,0:T(8,128)(2,1)} %slice.55) | data formatting | bytes 6291456 | tf_op jit(solution)/shard_map/reshape;reshape;squeeze | solution.py:208
  127.2 2.8 %slice-done = bf16[2,2,1536,512]{3,2,1,0:T(8,128)(2,1)S(1)} async-done(((bf16[3,2,1536,512]{3,2,1,0:T(8,128)(2,1)}), bf16[2,2,1536,512]{3,2,1,0:T(8,128)(2,1)S(1)}, s32[]{:S(2)}) %slice-start) | async-done | bytes 6291480 | tf_op jit(solution)/shard_map/slice | solution.py:204
  130.0 1.4 fusion.15
  131.4 0.2 fusion.37
  131.6 0.4 copy-done.19
  132.0 3.3 %bitcast_convert_fusion = bf16[512,768]{1,0:T(8,128)(2,1)} fusion(bf16[2,192,512]{2,1,0:T(8,128)(2,1)S(1)} %fusion.37, bf16[2,512,1536]{2,1,0:T(8,128)(2,1)} %reshape_reshape_squeeze.3, s32[]{:T(128)S(6)} %select_n.57, f32[2,192]{1,0:T(2,128)S(1)} %select_reduce_fusion, s32[2,512]{1,0:T(2,128)S(1)} %bitcast.121, pred[2,512]{1,0:T(4,128)(4,1)S(1)} %copy-done.21), kind=kOutput, calls=%fused_computation.17 | convolution fusion | flops 605356032 | bytes 2759172 | tf_op jit(solution)/shard_map/ect,ecd->td/dot_general | solution.py:282
  135.4 0.5 collective-permute-start.3
  137.6 3.8 %dynamic_update_slice.16 = bf16[1,4,2560,64]{2,3,1,0:T(8,128)(2,1)} dynamic-update-slice(bf16[1,4,2560,64]{2,3,1,0:T(8,128)(2,1)} %copy.59, bf16[1,4,512,64]{2,3,1,0:T(8,128)(2,1)S(1)} %pad_maximum_fusion.1, s32[]{:T(128)} %constant.50.clone.1, s32[]{:T(128)} %constant.50.clone.1, s32[]{:T(128)S(6)} %select_n.58, s32[]{:T(128)} %constant.50.clone.1) | dynamic-update-slice | bytes 524292 | tf_op jit(solution)/shard_map/dynamic_update_slice | solution.py:230
  141.4 3.8 %dynamic_update_slice.17 = bf16[1,4,2560,64]{2,3,1,0:T(8,128)(2,1)} dynamic-update-slice(bf16[1,4,2560,64]{2,3,1,0:T(8,128)(2,1)} %copy.60, bf16[1,4,512,64]{2,3,1,0:T(8,128)(2,1)S(1)} %bitcast.113, s32[]{:T(128)} %constant.50.clone.1, s32[]{:T(128)} %constant.50.clone.1, s32[]{:T(128)S(6)} %select_n.58, s32[]{:T(128)} %constant.50.clone.1) | dynamic-update-slice | bytes 524292 | tf_op jit(solution)/shard_map/dynamic_update_slice | solution.py:231
  145.2 7.7 %collective-permute-done.3 = bf16[512,768]{1,0:T(8,128)(2,1)} collective-permute-done((bf16[512,768]{1,0:T(8,128)(2,1)}, bf16[512,768]{1,0:T(8,128)(2,1)}, u32[]{:S(2)}, u32[]{:S(2)}) %collective-permute-start.3) | collective-permute-done | bytes 786464 | tf_op jit(solution)/shard_map/ppermute | solution.py:145
  152.9 4.0 %fusion.30 = bf16[1,512,768]{2,1,0:T(8,128)(2,1)} fusion(bf16[512,768]{1,0:T(8,128)(2,1)} %collective-permute-done.3, f32[512,1536]{1,0:T(8,128)} %copy-done.4, s32[]{:T(128)S(6)} %select_n.53, bf16[2,192,512]{2,1,0:T(8,128)(2,1)S(1)} %fusion.37, bf16[2,512,1536]{2,1,0:T(8,128)(2,1)} %reshape_reshape_squeeze.3, f32[2,192]{1,0:T(2,128)S(1)} %select_reduce_fusion, ...), kind=kOutput, calls=%fused_computation.33 | convolution fusion | flops 607322112 | bytes 5119488 | tf_op jit(solution)/shard_map/ect,ecd->td/dot_general | solution.py:282
  (62 shorter events, 0.3 us)
Async XLA Ops:
  7.2 62.7 %copy-start = (bf16[768,1536]{1,0:T(8,128)(2,1)S(1)}, bf16[768,1536]{1,0:T(8,128)(2,1)}, u32[]{:S(2)}) copy-start(bf16[768,1536]{1,0:T(8,128)(2,1)} %param.28) | copy-start | bytes 7077892
  7.2 110.4 %all-gather.2.cloned.1.call-start = ((), (), s32[]{:S(2)}) async-start(), calls=%async_computation | async-start | bytes 10027008 | tf_op jit(solution)/shard_map/all_gather | solution.py:198
  7.2 2.6 %copy-start.7 = (bf16[1,4,2560,64]{2,3,1,0:T(8,128)(2,1)S(1)}, bf16[1,4,2560,64]{2,3,1,0:T(8,128)(2,1)}, u32[]{:S(2)}) copy-start(bf16[1,4,2560,64]{2,3,1,0:T(8,128)(2,1)} %param.18) | copy-start | bytes 3932164
  9.9 2.2 %copy-start.14 = (bf16[2,96,512]{2,1,0:T(8,128)(2,1)S(1)}, bf16[2,96,512]{2,1,0:T(8,128)(2,1)}, u32[]{:S(2)}) copy-start(bf16[2,96,512]{2,1,0:T(8,128)(2,1)} %param.30) | copy-start | bytes 589828
  10.9 3.0 %copy-start.12 = (bf16[1,512,768]{2,1,0:T(8,128)(2,1)S(1)}, bf16[1,512,768]{2,1,0:T(8,128)(2,1)}, u32[]{:S(2)}) copy-start(bf16[1,512,768]{2,1,0:T(8,128)(2,1)} %param.16) | copy-start | bytes 2359300
  10.9 4.6 %copy-start.15 = (s32[1,512,8]{1,2,0:T(8,128)S(1)}, s32[1,512,8]{1,2,0:T(8,128)}, u32[]{:S(2)}) copy-start(s32[1,512,8]{1,2,0:T(8,128)} %param.21) | copy-start | bytes 49156
  13.9 19.5 %collective-permute-start = (bf16[512,768]{1,0:T(8,128)(2,1)S(1)}, bf16[512,768]{1,0:T(8,128)(2,1)}, u32[]{:S(2)}, u32[]{:S(2)}) collective-permute-start(bf16[512,768]{1,0:T(8,128)(2,1)S(1)} %bitcast.105), channel_id=1, source_target_pairs={{0,1},{1,0},{2,3},{3,2},{4,5},{5,4},{6,7},{7,6},{8,9},{9,8},{10,11... | collective-permute-start | bytes 2359304 | tf_op jit(solution)/shard_map/ppermute | solution.py:145
  15.5 0.6 copy-start.24
  16.0 0.6 copy-start.16
  22.6 12.3 %copy-start.26 = (bf16[1536,768]{1,0:T(8,128)(2,1)S(1)}, bf16[1536,768]{1,0:T(8,128)(2,1)}, u32[]{:S(2)}) copy-start(bf16[1536,768]{1,0:T(8,128)(2,1)} %param.25) | copy-start | bytes 7077892
  22.6 12.3 %copy-start.28 = (f32[1536]{0:T(1024)S(1)}, f32[1536]{0:T(1024)}, u32[]{:S(2)}) copy-start(f32[1536]{0:T(1024)} %param.23) | copy-start | bytes 18436
  34.5 2.0 %copy-start.1 = (bf16[512,1536]{1,0:T(8,128)(2,1)}, bf16[512,1536]{1,0:T(8,128)(2,1)S(1)}, u32[]{:S(2)}) copy-start(bf16[512,1536]{1,0:T(8,128)(2,1)S(1)} %constant_dynamic-update-slice_fusion) | copy-start | bytes 4718596
  39.8 4.1 %copy-start.5 = (bf16[4,3,512,32]{3,2,1,0:T(8,128)(2,1)S(1)}, bf16[4,3,512,32]{3,2,1,0:T(8,128)(2,1)}, u32[]{:S(2)}) copy-start(bf16[4,3,512,32]{3,2,1,0:T(8,128)(2,1)} %copy.38) | copy-start | bytes 1179652
  39.8 4.1 %copy-start.6 = (bf16[4,3,512,32]{3,2,1,0:T(8,128)(2,1)S(1)}, bf16[4,3,512,32]{3,2,1,0:T(8,128)(2,1)}, u32[]{:S(2)}) copy-start(bf16[4,3,512,32]{3,2,1,0:T(8,128)(2,1)} %copy.37) | copy-start | bytes 1179652
  42.5 0.7 copy-start.8
  42.5 0.7 copy-start.10
  44.9 2.0 %copy-start.2 = (bf16[512,1536]{1,0:T(8,128)(2,1)S(1)}, bf16[512,1536]{1,0:T(8,128)(2,1)}, u32[]{:S(2)}) copy-start(bf16[512,1536]{1,0:T(8,128)(2,1)} %copy-done.1) | copy-start | bytes 4718596
  44.9 2.2 %copy-start.27 = (bf16[1536,256]{1,0:T(8,128)(2,1)S(1)}, bf16[1536,256]{1,0:T(8,128)(2,1)}, u32[]{:S(2)}) copy-start(bf16[1536,256]{1,0:T(8,128)(2,1)} %param.27) | copy-start | bytes 2359300
  69.9 2.4 %copy-start.17 = (s32[512,2]{0,1:T(2,128)S(1)}, s32[512,2]{0,1:T(2,128)}, u32[]{:S(2)}) copy-start(s32[512,2]{0,1:T(2,128)} %copy-done.16) | copy-start | bytes 12292
  70.7 26.2 %collective-permute-start.2 = (bf16[256,1536]{1,0:T(8,128)(2,1)S(1)}, bf16[256,1536]{1,0:T(8,128)(2,1)}, u32[]{:S(2)}, u32[]{:S(2)}) collective-permute-start(bf16[256,1536]{1,0:T(8,128)(2,1)S(1)} %convolution_convert_fusion.1), channel_id=1, source_target_pairs={{0,1},{1,0},{2,3},{3,2},{4,5},{5,4},{6,7},{7,6},{8,9},{9,8},{10,11... | collective-permute-start | bytes 2359304 | tf_op jit(solution)/shard_map/ppermute | solution.py:145
  95.1 1.4 copy-start.22
  95.1 1.4 copy-start.25
  95.2 1.5 copy-start.18
  95.2 1.5 copy-start.20
  96.0 18.2 %collective-permute-start.1 = (bf16[256,1536]{1,0:T(8,128)(2,1)S(1)}, bf16[256,1536]{1,0:T(8,128)(2,1)S(1)}, u32[]{:S(2)}, u32[]{:S(2)}) collective-permute-start(bf16[256,1536]{1,0:T(8,128)(2,1)S(1)} %convolution_convert_fusion.2), channel_id=1, source_target_pairs={{0,1},{1,0},{2,3},{3,2},{4,5},{5,4},{6,7},{7,6},{8,9},{9,8},{10,11... | collective-permute-start | bytes 2359304 | tf_op jit(solution)/shard_map/ppermute | solution.py:145
  98.3 16.1 %copy-start.3 = (bf16[512,1536]{1,0:T(8,128)(2,1)S(1)}, bf16[512,1536]{1,0:T(8,128)(2,1)}, u32[]{:S(2)}) copy-start(bf16[512,1536]{1,0:T(8,128)(2,1)} %copy-done.1) | copy-start | bytes 4718596
  114.4 2.2 %copy-start.23 = (f32[1536]{0:T(1024)S(1)}, f32[1536]{0:T(1024)}, u32[]{:S(2)}) copy-start(f32[1536]{0:T(1024)} %param.24) | copy-start | bytes 18436
  114.9 1.7 %copy-start.4 = (f32[512,1536]{1,0:T(8,128)}, f32[512,1536]{1,0:T(8,128)S(1)}, u32[]{:S(2)}) copy-start(f32[512,1536]{1,0:T(8,128)S(1)} %get-tuple-element.12) | copy-start | bytes 9437188
  127.2 2.8 %slice-start = ((bf16[3,2,1536,512]{3,2,1,0:T(8,128)(2,1)}), bf16[2,2,1536,512]{3,2,1,0:T(8,128)(2,1)S(1)}, s32[]{:S(2)}) async-start(bf16[3,2,1536,512]{3,2,1,0:T(8,128)(2,1)} %all-gather.2.cloned.1.call-done), calls=%async_computation.1 | async-start | bytes 12582912 | tf_op jit(solution)/shard_map/slice | solution.py:204
  131.3 0.7 copy-start.19
  131.3 0.7 copy-start.21
  132.0 5.5 %copy-start.9 = (bf16[4,512,32]{1,2,0:T(8,128)(2,1)S(1)}, bf16[4,512,32]{1,2,0:T(8,128)(2,1)}, u32[]{:S(2)}) copy-start(bf16[4,512,32]{1,2,0:T(8,128)(2,1)} %copy-done.8) | copy-start | bytes 393220
  132.0 5.6 %copy-start.11 = (bf16[4,512,32]{1,2,0:T(8,128)(2,1)S(1)}, bf16[4,512,32]{1,2,0:T(8,128)(2,1)}, u32[]{:S(2)}) copy-start(bf16[4,512,32]{1,2,0:T(8,128)(2,1)} %copy-done.10) | copy-start | bytes 393220
  132.0 9.4 %copy-start.13 = (bf16[512,256]{0,1:T(8,128)(2,1)S(1)}, bf16[512,256]{0,1:T(8,128)(2,1)}, u32[]{:S(2)}) copy-start(bf16[512,256]{0,1:T(8,128)(2,1)} %convolution_convert_fusion.3) | copy-start | bytes 786436
  135.4 17.5 %collective-permute-start.3 = (bf16[512,768]{1,0:T(8,128)(2,1)}, bf16[512,768]{1,0:T(8,128)(2,1)}, u32[]{:S(2)}, u32[]{:S(2)}) collective-permute-start(bf16[512,768]{1,0:T(8,128)(2,1)} %bitcast_convert_fusion), channel_id=1, source_target_pairs={{0,1},{1,0},{2,3},{3,2},{4,5},{5,4},{6,7},{7,6},{8,9},{9,8},{10,11... | collective-permute-start | bytes 2359304 | tf_op jit(solution)/shard_map/ppermute | solution.py:145
Sparse Core Ops, SparseCore 0:
  14.0 81.5 all-gather.1

commit v3 on v1

--- a/solution.py
+++ b/solution.py
@@ -44,6 +44,7 @@
     cached = keys.shape[2] - block
     wide = cached if cached % block == 0 else block
     blocks = 1 + cached // wide
+    seen = first_token + tokens if (first_token + tokens) % 128 == 0 else block
 
     def cached_blocks(length_ref):
         return (length_ref[0] + wide - 1) // wide
@@ -81,7 +82,7 @@
 
         @pl.when(step == 0)
         def _():
-            shape = (rows, block)
+            shape = (rows, seen)
             column = lax.broadcasted_iota(jnp.int32, shape, 1)
             token = first_token + lax.rem(lax.broadcasted_iota(jnp.int32, shape, 0), tokens)
             visit(kn_ref[0], vn_ref[0], column <= token, True)
@@ -116,8 +117,8 @@
             pl.BlockSpec((1, rows, head_dim), fixed_map),
             pl.BlockSpec((1, head_dim, wide), cache_map),
             pl.BlockSpec((1, head_dim, wide), cache_map),
-            pl.BlockSpec((1, head_dim, block), fixed_map),
-            pl.BlockSpec((1, head_dim, block), fixed_map),
+            pl.BlockSpec((1, head_dim, seen), fixed_map),
+            pl.BlockSpec((1, head_dim, seen), fixed_map),
         ],
         out_specs=pl.BlockSpec((1, rows, head_dim), fixed_map),
         scratch_shapes=[

time: 158 us -> 158 us (level)
  waiting for transfers between devices: 43.4 us -> 37.4 us
  Pallas kernels: 36 us -> 40 us
  local copies, waits for them, and re-layouts: 23.8 us -> 26 us
    pallas_call x2, Pallas kernels: 36 us -> 40 us  [flash_attend(): pl.pallas_call(kernel, grid_spec=grid_spec, out_shape=jax.ShapeDtypeStruc...]
    all_gather x1, waiting for transfers between devices: 4 us -> 0.29 us  [on_device(): down_whole = lax.all_gather(expert_down, 'req', axis=1, tiled=True)]
    ppermute x4, waiting for transfers between devices: 39.3 us -> 37.1 us  [shifted(): lax.ppermute(values, 'ep', [(i, (i + shift) % devices) for i in range(dev...]
  transfers between devices with their start and end apart: 6 -> 6, of which waited for: 4 -> 4; matrix products, arithmetic and copies ran while one was open for 24% -> 26% of each run, Pallas kernels for 23% -> 26%
where the time goes in v3:
time: 158 us; the launch traced here: 155 us
  Pallas kernels  40 us (25%)
  waiting for transfers between devices  37.4 us (24%)
  local copies, waits for them, and re-layouts  26 us (16%)
  matrix products  19.6 us (12%)
  between operations  16.4 us (10%)
  other arithmetic  10.8 us (7%)
  starting transfers between devices  5.13 us (3%)
    pallas_call x2, Pallas kernels, flash_attend(): pl.pallas_call(kernel, grid_spec=grid_spec, out_shape=jax.ShapeDtypeStruc...  40 us
    ppermute x4, waiting for transfers between devices, shifted(): lax.ppermute(values, 'ep', [(i, (i + shift) % devices) for i in range(dev...  37.1 us
    unnamed x67, local copies, waits for them, and re-layouts  9.8 us
    dot_general x2, matrix products, expert_block(): jnp.einsum('ect,ecd->td', table, contrib, preferred_element_type=jnp.floa...  7.24 us
    ppermute x4, starting transfers between devices, shifted(): lax.ppermute(values, 'ep', [(i, (i + shift) % devices) for i in range(dev...  5.05 us
    dot_general x1, matrix products, on_device(): jnp.einsum('ecd,kedf->kecf', dispatched, gate_up, preferred_element_type=...  4.21 us
    dynamic_update_slice x1, local copies, waits for them, and re-layouts, on_device(): keys = lax.dynamic_update_slice(key_cache[0], key_new, (zero, length, zero))  3.8 us
    dynamic_update_slice x1, local copies, waits for them, and re-layouts, on_device(): lax.dynamic_update_slice(value_cache[0], value_new, (zero, length, zero))  3.78 us
  transfers between devices with their start and end apart: 6, of which 4 were waited for; matrix products, arithmetic and copies ran while one was open for 26% of the time, Pallas kernels for 26%

profile of v3, /device:TPU:16, one launch (start us, length us, event | category | flops | bytes accessed | tf_op | source)
XLA Modules:
  0.0 155.3 jit_solution(5449904828466715137)
XLA Ops:
  7.2 2.6 %copy.60 = bf16[1,4,2560,64]{2,3,1,0:T(8,128)(2,1)} copy(bf16[1,4,2560,64]{2,3,1,0:T(8,128)(2,1)} %param.18) | data formatting | bytes 2621440
  9.9 1.1 copy.59
  11.0 0.2 copy-done.15
  11.2 0.8 pad_maximum_fusion
  12.0 0.0 all-gather.3.cloned.1.call-start
  12.0 1.6 %collective-permute-start = (bf16[512,768]{1,0:T(8,128)(2,1)S(1)}, bf16[512,768]{1,0:T(8,128)(2,1)}, u32[]{:S(2)}, u32[]{:S(2)}) collective-permute-start(bf16[512,768]{1,0:T(8,128)(2,1)S(1)} %bitcast.103), channel_id=1, source_target_pairs={{0,1},{1,0},{2,3},{3,2},{4,5},{5,4},{6,7},{7,6},{8,9},{9,8},{10,11... | collective-permute-start | bytes 2359304 | tf_op jit(solution)/shard_map/ppermute | solution.py:146
  13.7 0.6 fusion.56
  14.3 1.3 fusion.57
  15.6 0.6 add_convert_fusion.3
  16.3 0.1 fusion.50
  16.4 0.5 copy-done.25
  16.8 0.6 copy-done.17
  17.4 0.6 reduce-window.6
  18.0 0.2 slice_reduce_fusion
  18.3 0.2 reduce-window.9
  18.5 0.7 add_bitcast_fusion
  19.1 0.3 multiply_cosine_fusion
  19.4 0.1 broadcast_in_dim.33
  19.6 0.1 constant_dynamic-update-slice_fusion.1
  19.6 11.8 %collective-permute-done = bf16[512,768]{1,0:T(8,128)(2,1)} collective-permute-done((bf16[512,768]{1,0:T(8,128)(2,1)S(1)}, bf16[512,768]{1,0:T(8,128)(2,1)}, u32[]{:S(2)}, u32[]{:S(2)}) %collective-permute-start) | collective-permute-done | bytes 786464 | tf_op jit(solution)/shard_map/ppermute | solution.py:146
  31.5 1.2 constant_dynamic-update-slice_fusion
  32.7 0.4 fusion.2
  33.1 1.6 %fusion.61 = f32[512,768]{0,1:T(8,128)S(1)} fusion(bf16[1536,768]{1,0:T(8,128)(2,1)S(1)} %copy-done.27, bf16[512,1536]{1,0:T(8,128)(2,1)S(1)} %constant_dynamic-update-slice_fusion, f32[1536]{0:T(1024)S(1)} %copy-done.29, f32[512]{0:T(512)S(1)} %add_rsqrt_fusion.1), kind=kOutput, calls=%fused_computation.82 | convolution fusion | flops 1211105280 | bytes 5513216 | tf_op jit(solution)/shard_map/dot_general | solution.py:205
  34.7 0.3 subtract_convert_fusion
  34.9 1.5 copy.37
  36.5 1.5 copy.38
  38.0 2.5 %fusion.59 = f32[512,256]{0,1:T(8,128)S(1)} fusion(bf16[1536,256]{1,0:T(8,128)(2,1)} %param.26, bf16[512,1536]{1,0:T(8,128)(2,1)} %copy-done.1, f32[1536]{0:T(1024)S(1)} %copy-done.29, f32[512]{0:T(512)S(1)} %add_rsqrt_fusion.1), kind=kOutput, calls=%fused_computation.81 | convolution fusion | flops 405798912 | bytes 2891776 | tf_op jit(solution)/shard_map/dot_general | solution.py:206
  40.5 0.1 subtract_convert_fusion.1
  40.6 0.6 copy-done.8
  41.2 0.0 copy-done.10
  41.3 0.7 maximum_bitcast_fusion.kn_ref
  42.0 1.0 maximum_multiply_fusion
  43.0 1.2 fusion.64
  44.2 0.8 copy-done.2
  45.0 0.2 copy-done.28
  45.2 1.5 convolution_convert_fusion.3
  46.7 19.9 %shard_map.175 = bf16[4,768,64]{2,1,0:T(8,128)(2,1)} custom-call(s32[1]{0:T(128)} %bitcast.1.length_ref, bf16[4,768,64]{2,1,0:T(8,128)(2,1)} %bitcast.107, bf16[4,64,2560]{2,1,0:T(8,128)(2,1)} %bitcast.99, bf16[4,64,2560]{2,1,0:T(8,128)(2,1)} %bitcast.97, bf16[4,64,512]{2,1,0:T(8,128)(2,1)} %maximum_bitcast_fusion.kn_ref, bf16[4,64,512]{2,1,0:T(8,128)(2,1)} %bitcast.109), custom_call_target="tpu_custom_call" | custom-call | flops 2013265920 | bytes 3407872 | tf_op jit(solution)/shard_map/pallas_call | solution.py:131
  66.6 1.4 copy.39
  68.0 0.8 convolution_convert_fusion.2
  68.8 1.6 %collective-permute-start.1 = (bf16[256,1536]{1,0:T(8,128)(2,1)S(1)}, bf16[256,1536]{1,0:T(8,128)(2,1)}, u32[]{:S(2)}, u32[]{:S(2)}) collective-permute-start(bf16[256,1536]{1,0:T(8,128)(2,1)S(1)} %convolution_convert_fusion.2), channel_id=1, source_target_pairs={{0,1},{1,0},{2,3},{3,2},{4,5},{5,4},{6,7},{7,6},{8,9},{9,8},{10,11... | collective-permute-start | bytes 2359304 | tf_op jit(solution)/shard_map/ppermute | solution.py:146
  70.4 0.6 broadcast_compare_fusion
  71.0 1.3 copy.52
  72.2 20.1 %shard_map.176 = bf16[4,768,64]{2,1,0:T(8,128)(2,1)} custom-call(s32[1]{0:T(128)} %bitcast.1.length_ref, bf16[4,768,64]{2,1,0:T(8,128)(2,1)} %bitcast.106, bf16[4,64,2560]{2,1,0:T(8,128)(2,1)} %bitcast.100, bf16[4,64,2560]{2,1,0:T(8,128)(2,1)} %bitcast.98, bf16[4,64,512]{2,1,0:T(8,128)(2,1)} %maximum_bitcast_fusion.kn_ref, bf16[4,64,512]{2,1,0:T(8,128)(2,1)} %bitcast.110), custom_call_target="tpu_custom_call" | custom-call | flops 2013265920 | bytes 3407872 | tf_op jit(solution)/shard_map/pallas_call | solution.py:131
  92.4 1.4 copy.40
  93.8 0.8 convolution_convert_fusion.1
  94.6 0.5 collective-permute-start.2
  95.1 0.1 fusion.51
  95.2 0.2 select_reduce_fusion
  95.5 1.3 convert_add_fusion.2
  96.9 16.2 %collective-permute-done.2 = bf16[256,1536]{1,0:T(8,128)(2,1)S(1)} collective-permute-done((bf16[256,1536]{1,0:T(8,128)(2,1)S(1)}, bf16[256,1536]{1,0:T(8,128)(2,1)S(1)}, u32[]{:S(2)}, u32[]{:S(2)}) %collective-permute-start.2) | collective-permute-done | bytes 786464 | tf_op jit(solution)/shard_map/ppermute | solution.py:146
  113.0 0.2 convert_add_fusion.1
  113.3 0.5 multiply_reduce_fusion
  113.8 1.6 %copy-done.4 = f32[512,1536]{1,0:T(8,128)} copy-done((f32[512,1536]{1,0:T(8,128)}, f32[512,1536]{1,0:T(8,128)S(1)}, u32[]{:S(2)}) %copy-start.4) | copy-done | bytes 3145752
  115.4 1.0 convolution_convert_fusion
  116.4 4.2 %fusion.15 = f32[2,2,192,512]{3,2,0,1:T(8,128)S(1)} fusion(bf16[2,2,1536,512]{3,2,1,0:T(8,128)(2,1)} %all-gather.5.cloned.1.call-done, bf16[2,192,1536]{2,1,0:T(8,128)(2,1)S(1)} %convolution_convert_fusion), kind=kOutput, calls=%fused_computation.28 | convolution fusion | flops 1207959552 | bytes 9043968 | tf_op jit(solution)/shard_map/ecd,kedf->kecf/dot_general | solution.py:262
  120.7 0.2 fusion.37
  120.9 0.3 all-gather.3.cloned.1.call-done
  121.2 0.1 copy-done.20
  121.3 3.3 %bitcast_convert_fusion = bf16[512,768]{1,0:T(8,128)(2,1)} fusion(bf16[2,192,512]{2,1,0:T(8,128)(2,1)S(1)} %fusion.37, bf16[2,512,1536]{2,1,0:T(8,128)(2,1)} %all-gather.3.cloned.1.call-done, s32[]{:T(128)S(6)} %select_n.57, f32[2,192]{1,0:T(2,128)S(1)} %select_reduce_fusion, s32[2,512]{1,0:T(2,128)S(1)} %bitcast.119, pred[2,512]{1,0:T(4,128)(4,1)S(1)} %copy-done.22), kind=kOutput, calls=%fused_computation.17 | convolution fusion | flops 605356032 | bytes 2759172 | tf_op jit(solution)/shard_map/ect,ecd->td/dot_general | solution.py:271
  124.6 1.4 collective-permute-start.3
  127.9 3.8 %dynamic_update_slice.16 = bf16[1,4,2560,64]{2,3,1,0:T(8,128)(2,1)} dynamic-update-slice(bf16[1,4,2560,64]{2,3,1,0:T(8,128)(2,1)} %copy.59, bf16[1,4,512,64]{2,3,1,0:T(8,128)(2,1)S(1)} %pad_maximum_fusion.1, s32[]{:T(128)} %constant.50.clone.1, s32[]{:T(128)} %constant.50.clone.1, s32[]{:T(128)S(6)} %select_n.58, s32[]{:T(128)} %constant.50.clone.1) | dynamic-update-slice | bytes 524292 | tf_op jit(solution)/shard_map/dynamic_update_slice | solution.py:219
  131.7 3.8 %dynamic_update_slice.17 = bf16[1,4,2560,64]{2,3,1,0:T(8,128)(2,1)} dynamic-update-slice(bf16[1,4,2560,64]{2,3,1,0:T(8,128)(2,1)} %copy.60, bf16[1,4,512,64]{2,3,1,0:T(8,128)(2,1)S(1)} %bitcast.111, s32[]{:T(128)} %constant.50.clone.1, s32[]{:T(128)} %constant.50.clone.1, s32[]{:T(128)S(6)} %select_n.58, s32[]{:T(128)} %constant.50.clone.1) | dynamic-update-slice | bytes 524292 | tf_op jit(solution)/shard_map/dynamic_update_slice | solution.py:220
  135.4 9.1 %collective-permute-done.3 = bf16[512,768]{1,0:T(8,128)(2,1)} collective-permute-done((bf16[512,768]{1,0:T(8,128)(2,1)}, bf16[512,768]{1,0:T(8,128)(2,1)}, u32[]{:S(2)}, u32[]{:S(2)}) %collective-permute-start.3) | collective-permute-done | bytes 786464 | tf_op jit(solution)/shard_map/ppermute | solution.py:146
  144.5 4.0 %fusion.30 = bf16[1,512,768]{2,1,0:T(8,128)(2,1)} fusion(bf16[512,768]{1,0:T(8,128)(2,1)} %collective-permute-done.3, f32[512,1536]{1,0:T(8,128)} %copy-done.4, s32[]{:T(128)S(6)} %select_n.53, bf16[2,192,512]{2,1,0:T(8,128)(2,1)S(1)} %fusion.37, bf16[2,512,1536]{2,1,0:T(8,128)(2,1)} %all-gather.3.cloned.1.call-done, f32[2,192]{1,0:T(2,128)S(1)} %select_reduce_fusion, ...), kind=kOutput, calls=%fused_computation.33 | convolution fusion | flops 607322112 | bytes 5119488 | tf_op jit(solution)/shard_map/ect,ecd->td/dot_general | solution.py:271
  (66 shorter events, 0.3 us)
Async XLA Ops:
  7.2 60.8 %copy-start = (bf16[768,1536]{1,0:T(8,128)(2,1)S(1)}, bf16[768,1536]{1,0:T(8,128)(2,1)}, u32[]{:S(2)}) copy-start(bf16[768,1536]{1,0:T(8,128)(2,1)} %param.28) | copy-start | bytes 7077892
  7.2 109.2 %all-gather.5.cloned.1.call-start = ((), (), s32[]{:S(2)}) async-start(), calls=%async_computation.1 | async-start | bytes 6684672 | tf_op jit(solution)/shard_map/all_gather | solution.py:197
  7.2 2.6 %copy-start.7 = (bf16[1,4,2560,64]{2,3,1,0:T(8,128)(2,1)S(1)}, bf16[1,4,2560,64]{2,3,1,0:T(8,128)(2,1)}, u32[]{:S(2)}) copy-start(bf16[1,4,2560,64]{2,3,1,0:T(8,128)(2,1)} %param.17) | copy-start | bytes 3932164
  9.9 1.1 copy-start.14
  9.9 1.3 copy-start.15
  9.9 2.2 %copy-start.12 = (bf16[1,512,768]{2,1,0:T(8,128)(2,1)S(1)}, bf16[1,512,768]{2,1,0:T(8,128)(2,1)}, u32[]{:S(2)}) copy-start(bf16[1,512,768]{2,1,0:T(8,128)(2,1)} %param.16) | copy-start | bytes 2359300
  9.9 3.8 %copy-start.30 = (s32[16]{0:T(128)S(1)}, s32[16]{0:T(128)}, u32[]{:S(2)}) copy-start(s32[16]{0:T(128)} %param.19) | copy-start | bytes 196
  9.9 4.4 %copy-start.31 = (s32[16]{0:T(128)S(1)}, s32[16]{0:T(128)}, u32[]{:S(2)}) copy-start(s32[16]{0:T(128)} %param.20) | copy-start | bytes 196
  9.9 6.4 %copy-start.16 = (s32[1,512,8]{1,2,0:T(8,128)S(1)}, s32[1,512,8]{1,2,0:T(8,128)}, u32[]{:S(2)}) copy-start(s32[1,512,8]{1,2,0:T(8,128)} %param.21) | copy-start | bytes 49156
  12.0 109.3 %all-gather.3.cloned.1.call-start = ((), (), s32[]{:S(2)}) async-start(), calls=%async_computation | async-start | bytes 3342336 | tf_op jit(solution)/shard_map/all_gather | solution.py:198
  12.0 19.5 %collective-permute-start = (bf16[512,768]{1,0:T(8,128)(2,1)S(1)}, bf16[512,768]{1,0:T(8,128)(2,1)}, u32[]{:S(2)}, u32[]{:S(2)}) collective-permute-start(bf16[512,768]{1,0:T(8,128)(2,1)S(1)} %bitcast.103), channel_id=1, source_target_pairs={{0,1},{1,0},{2,3},{3,2},{4,5},{5,4},{6,7},{7,6},{8,9},{9,8},{10,11... | collective-permute-start | bytes 2359304 | tf_op jit(solution)/shard_map/ppermute | solution.py:146
  16.3 0.6 copy-start.25
  16.8 0.6 copy-start.17
  19.6 13.5 %copy-start.27 = (bf16[1536,768]{1,0:T(8,128)(2,1)S(1)}, bf16[1536,768]{1,0:T(8,128)(2,1)}, u32[]{:S(2)}) copy-start(bf16[1536,768]{1,0:T(8,128)(2,1)} %param.25) | copy-start | bytes 7077892
  19.6 13.5 %copy-start.29 = (f32[1536]{0:T(1024)S(1)}, f32[1536]{0:T(1024)}, u32[]{:S(2)}) copy-start(f32[1536]{0:T(1024)} %param.23) | copy-start | bytes 18436
  32.7 2.0 %copy-start.1 = (bf16[512,1536]{1,0:T(8,128)(2,1)}, bf16[512,1536]{1,0:T(8,128)(2,1)S(1)}, u32[]{:S(2)}) copy-start(bf16[512,1536]{1,0:T(8,128)(2,1)S(1)} %constant_dynamic-update-slice_fusion) | copy-start | bytes 4718596
  37.9 4.0 %copy-start.5 = (bf16[4,3,512,32]{3,2,1,0:T(8,128)(2,1)S(1)}, bf16[4,3,512,32]{3,2,1,0:T(8,128)(2,1)}, u32[]{:S(2)}) copy-start(bf16[4,3,512,32]{3,2,1,0:T(8,128)(2,1)} %copy.37) | copy-start | bytes 1179652
  38.0 4.1 %copy-start.6 = (bf16[4,3,512,32]{3,2,1,0:T(8,128)(2,1)S(1)}, bf16[4,3,512,32]{3,2,1,0:T(8,128)(2,1)}, u32[]{:S(2)}) copy-start(bf16[4,3,512,32]{3,2,1,0:T(8,128)(2,1)} %copy.38) | copy-start | bytes 1179652
  40.6 0.7 copy-start.8
  40.6 0.7 copy-start.10
  43.0 2.1 %copy-start.2 = (bf16[512,1536]{1,0:T(8,128)(2,1)S(1)}, bf16[512,1536]{1,0:T(8,128)(2,1)}, u32[]{:S(2)}) copy-start(bf16[512,1536]{1,0:T(8,128)(2,1)} %copy-done.1) | copy-start | bytes 4718596
  43.0 2.3 %copy-start.28 = (bf16[1536,256]{1,0:T(8,128)(2,1)S(1)}, bf16[1536,256]{1,0:T(8,128)(2,1)}, u32[]{:S(2)}) copy-start(bf16[1536,256]{1,0:T(8,128)(2,1)} %param.27) | copy-start | bytes 2359300
  68.0 2.4 %copy-start.18 = (s32[512,2]{0,1:T(2,128)S(1)}, s32[512,2]{0,1:T(2,128)}, u32[]{:S(2)}) copy-start(s32[512,2]{0,1:T(2,128)} %copy-done.17) | copy-start | bytes 12292
  68.8 26.7 %collective-permute-start.1 = (bf16[256,1536]{1,0:T(8,128)(2,1)S(1)}, bf16[256,1536]{1,0:T(8,128)(2,1)}, u32[]{:S(2)}, u32[]{:S(2)}) collective-permute-start(bf16[256,1536]{1,0:T(8,128)(2,1)S(1)} %convolution_convert_fusion.2), channel_id=1, source_target_pairs={{0,1},{1,0},{2,3},{3,2},{4,5},{5,4},{6,7},{7,6},{8,9},{9,8},{10,11... | collective-permute-start | bytes 2359304 | tf_op jit(solution)/shard_map/ppermute | solution.py:146
  93.8 1.4 copy-start.23
  93.8 1.4 copy-start.26
  93.8 1.5 copy-start.19
  93.8 1.4 copy-start.21
  94.6 18.4 %collective-permute-start.2 = (bf16[256,1536]{1,0:T(8,128)(2,1)S(1)}, bf16[256,1536]{1,0:T(8,128)(2,1)S(1)}, u32[]{:S(2)}, u32[]{:S(2)}) collective-permute-start(bf16[256,1536]{1,0:T(8,128)(2,1)S(1)} %convolution_convert_fusion.1), channel_id=1, source_target_pairs={{0,1},{1,0},{2,3},{3,2},{4,5},{5,4},{6,7},{7,6},{8,9},{9,8},{10,11... | collective-permute-start | bytes 2359304 | tf_op jit(solution)/shard_map/ppermute | solution.py:146
  96.8 16.4 %copy-start.3 = (bf16[512,1536]{1,0:T(8,128)(2,1)S(1)}, bf16[512,1536]{1,0:T(8,128)(2,1)}, u32[]{:S(2)}) copy-start(bf16[512,1536]{1,0:T(8,128)(2,1)} %copy-done.1) | copy-start | bytes 4718596
  113.3 2.2 %copy-start.24 = (f32[1536]{0:T(1024)S(1)}, f32[1536]{0:T(1024)}, u32[]{:S(2)}) copy-start(f32[1536]{0:T(1024)} %param.24) | copy-start | bytes 18436
  113.8 1.7 %copy-start.4 = (f32[512,1536]{1,0:T(8,128)}, f32[512,1536]{1,0:T(8,128)S(1)}, u32[]{:S(2)}) copy-start(f32[512,1536]{1,0:T(8,128)S(1)} %get-tuple-element.12) | copy-start | bytes 9437188
  120.7 0.7 copy-start.20
  120.7 0.7 copy-start.22
  120.9 6.9 %copy-start.9 = (bf16[4,512,32]{1,2,0:T(8,128)(2,1)S(1)}, bf16[4,512,32]{1,2,0:T(8,128)(2,1)}, u32[]{:S(2)}) copy-start(bf16[4,512,32]{1,2,0:T(8,128)(2,1)} %copy-done.8) | copy-start | bytes 393220
  120.9 6.9 %copy-start.11 = (bf16[4,512,32]{1,2,0:T(8,128)(2,1)S(1)}, bf16[4,512,32]{1,2,0:T(8,128)(2,1)}, u32[]{:S(2)}) copy-start(bf16[4,512,32]{1,2,0:T(8,128)(2,1)} %copy-done.10) | copy-start | bytes 393220
  120.9 10.7 %copy-start.13 = (bf16[512,256]{0,1:T(8,128)(2,1)S(1)}, bf16[512,256]{0,1:T(8,128)(2,1)}, u32[]{:S(2)}) copy-start(bf16[512,256]{0,1:T(8,128)(2,1)} %convolution_convert_fusion.3) | copy-start | bytes 786436
  124.6 19.9 %collective-permute-start.3 = (bf16[512,768]{1,0:T(8,128)(2,1)}, bf16[512,768]{1,0:T(8,128)(2,1)}, u32[]{:S(2)}, u32[]{:S(2)}) collective-permute-start(bf16[512,768]{1,0:T(8,128)(2,1)} %bitcast_convert_fusion), channel_id=1, source_target_pairs={{0,1},{1,0},{2,3},{3,2},{4,5},{5,4},{6,7},{7,6},{8,9},{9,8},{10,11... | collective-permute-start | bytes 2359304 | tf_op jit(solution)/shard_map/ppermute | solution.py:146
Sparse Core Ops, SparseCore 0:
  12.1 62.5 all-gather.4
  77.0 44.2 all-gather.2
